TPU v7x, 32 devices: a whole 2x2x4 slice. The times are simulated.
32 devices in a mesh: req: 8 (over y, x, core), tp: 4 (over z).
Axes of the slice: x: 2, y: 2, z: 4, core: 2. Of those that a mesh axis runs over, the one named last changes fastest.
Arguments:
- residual: bfloat16 [2048, 2048], P('req', 'tp'), may hold values from -0.29882812 to 0.29882812
- queries: bfloat16 [2048, 1280], P('req', 'tp'), may hold values from -6 to 6
- suffix_kv: bfloat16 [2048, 4, 256], P('req', 'tp'), may hold values from -4 to 4
- prefix_cache: bfloat16 [8192, 4, 256], P('req', 'tp'), may hold values from -6 to 6
- out_weight: bfloat16 [1280, 2048], P('tp'), may hold values from -0.15625 to 0.15625
- norm_gain: bfloat16 [2048], replicated, may hold values from 0.5 to 1.5
- next_query_weight: bfloat16 [2048, 1280], P(None, 'tp'), may hold values from -0.125 to 0.125
- lengths: int32 [8, 4], P('req'), may hold values from 1 to 128, 256 in all within a row
- tenant: int32 [8, 4], P('req'), may hold values from 0 to 3
- owners: int32 [4], replicated, may hold values from 0 to 7, as said below
Outputs:
- new_residual: bfloat16 [2048, 2048], P('req', 'tp')
- next_queries: bfloat16 [2048, 1280], P('req', 'tp')
Inputs may be any that keep to these rules, and one draw needn't show every extreme that they name: `lengths`: each device's 4 requests fill its 256 rows in order. `owners`: distinct.
All inputs are finite; a program needn't handle non-finite values.
Results may differ from a plain program's by a relative error of at most 0.0065.
Values may be sent and summed in bfloat16 or wider, within the bound.
No kernel may reach another device: no remote copies, remote signals or barrier semaphores. Data moves between devices by JAX's collectives and lax.ppermute only.
A program may use at most 64 MiB of HBM per device.

v0:
```python
import jax
import jax.numpy as jnp
from jax import lax
from jax.experimental import pallas as pl
from jax.experimental.pallas import tpu as pltpu
from jax.sharding import PartitionSpec as P

QH = 20
KVH = 5
HD = 64
TENANTS = 4
MOSTLEN = 128
GATHER_SLOTS_MAX = 16


def from_root(block, axis, source):
    block = jnp.where(lax.axis_index(axis) == source, block, jnp.zeros_like(block))
    return lax.psum(block, axis)


def pick_heads(pair_rows, select):
    split_pair = pair_rows.reshape(pair_rows.shape[0], 2, 2, HD)
    key_heads = jnp.einsum(
        "njd,hj->nhd", split_pair[:, :, 0], select, preferred_element_type=jnp.float32
    ).astype(jnp.bfloat16)
    value_heads = jnp.einsum(
        "njd,hj->nhd", split_pair[:, :, 1], select, preferred_element_type=jnp.float32
    ).astype(jnp.bfloat16)
    return (key_heads, value_heads)


def xor_permute(block, mask, n_req):
    pairs = [(source, source ^ mask) for source in range(n_req)]
    return lax.ppermute(block, "req", pairs)


def tenant_slots(own_slot, owners, n_req):
    if n_req <= GATHER_SLOTS_MAX and n_req % 2 == 0 and (n_req & (n_req - 1)) == 0:
        req_index = lax.axis_index("req")
        mine = [own_slot] + [
            xor_permute(own_slot, 2 * chip_mask, n_req) for chip_mask in range(1, n_req // 2)
        ]
        theirs = [xor_permute(block, 1, n_req) for block in mine]
        slots = jnp.concatenate(
            [block for pair in zip(mine, theirs) for block in pair], axis=0
        )
        chip_offset = (owners // 2) ^ (req_index // 2)
        other_core = (owners % 2) != (req_index % 2)
        return slots, 2 * chip_offset + other_core.astype(jnp.int32)
    blocks = [from_root(own_slot, "req", owners[tenant_id]) for tenant_id in range(TENANTS)]
    return jnp.concatenate(blocks, axis=0), jnp.arange(TENANTS, dtype=jnp.int32)


def attention_kernel(
    slot_ref, first_ref, start_ref, query_ref, prefix_ref, suffix_ref, row_ref, pair_ref, out_ref
):
    request = pl.program_id(0)
    first = first_ref[request]
    start = start_ref[request]
    spread = query_ref[...]
    pair_lanes = 2 * HD
    prefix_keys = prefix_ref[:, :pair_lanes]
    prefix_values = prefix_ref[:, pair_lanes:]
    suffix_keys = suffix_ref[:, :pair_lanes]
    suffix_values = suffix_ref[:, pair_lanes:]
    contract = (((1,), (1,)), ((), ()))
    prefix_scores = lax.dot_general(
        spread, prefix_keys, contract, preferred_element_type=jnp.float32
    )
    suffix_scores = lax.dot_general(
        spread, suffix_keys, contract, preferred_element_type=jnp.float32
    )
    key_position = first + lax.broadcasted_iota(jnp.int32, suffix_scores.shape, 1)
    query_position = first + row_ref[...]
    allowed = (key_position >= start) & (key_position <= query_position)
    suffix_scores = jnp.where(allowed, suffix_scores, -jnp.inf)
    row_top = jnp.maximum(
        jnp.max(prefix_scores, axis=1, keepdims=True),
        jnp.max(suffix_scores, axis=1, keepdims=True),
    )
    prefix_weights = jnp.exp(prefix_scores - row_top)
    suffix_weights = jnp.exp(suffix_scores - row_top)
    denominator = jnp.sum(prefix_weights, axis=1, keepdims=True) + jnp.sum(
        suffix_weights, axis=1, keepdims=True
    )
    accumulated = jnp.dot(
        prefix_weights.astype(jnp.bfloat16), prefix_values, preferred_element_type=jnp.float32
    ) + jnp.dot(
        suffix_weights.astype(jnp.bfloat16), suffix_values, preferred_element_type=jnp.float32
    )
    attended = accumulated / denominator
    first_pair = attended[:, :HD]
    second_pair = attended[:, HD:]
    out_ref[...] = jnp.where(pair_ref[...] > 0, second_pair, first_pair).astype(out_ref.dtype)


def window_attention(
    slot_index, firsts, starts, spread, slots, suffix_windows, query_rows, row_pairs, slot_rows
):
    requests, flat_rows, query_lanes = spread.shape
    window = suffix_windows.shape[1]
    lanes = slots.shape[1]
    grid_spec = pltpu.PrefetchScalarGridSpec(
        num_scalar_prefetch=3,
        grid=(requests,),
        in_specs=[
            pl.BlockSpec((None, flat_rows, query_lanes), lambda k, slot, first, start: (k, 0, 0)),
            pl.BlockSpec((slot_rows, lanes), lambda k, slot, first, start: (slot[k], 0)),
            pl.BlockSpec((None, window, lanes), lambda k, slot, first, start: (k, 0, 0)),
            pl.BlockSpec((flat_rows, 1), lambda k, slot, first, start: (0, 0)),
            pl.BlockSpec((flat_rows, 1), lambda k, slot, first, start: (0, 0)),
        ],
        out_specs=pl.BlockSpec((None, flat_rows, HD), lambda k, slot, first, start: (k, 0, 0)),
    )
    return pl.pallas_call(
        attention_kernel,
        grid_spec=grid_spec,
        out_shape=jax.ShapeDtypeStruct((requests, flat_rows, HD), jnp.bfloat16),
    )(slot_index, firsts, starts, spread, slots, suffix_windows, query_rows, row_pairs)


def xor_tp(block, mask, n_tp):
    pairs = [(source, source ^ mask) for source in range(n_tp)]
    return lax.ppermute(block, "tp", pairs)


def from_partners(block, n_tp):
    if n_tp == 4:
        near = xor_tp(block, 1, n_tp)
        across = xor_tp(block, 2, n_tp)
        return [block, near, across, xor_tp(across, 1, n_tp)]
    return [block] + [xor_tp(block, mask, n_tp) for mask in range(1, n_tp)]


def shifted(block, shift, n_tp):
    pairs = [(source, (source + shift) % n_tp) for source in range(n_tp)]
    return lax.ppermute(block, "tp", pairs)


def local(
    residual,
    queries,
    suffix_kv,
    prefix_cache,
    out_weight,
    norm_gain,
    next_query_weight,
    lengths,
    tenant,
    owners,
    n_req,
    n_tp,
):
    row_count = queries.shape[0]
    head_count = queries.shape[1] // HD
    width = residual.shape[1]
    tp_index = lax.axis_index("tp")

    weight_pieces = []
    for mask in range(n_tp):
        partner = tp_index ^ mask
        piece = lax.dynamic_slice_in_dim(out_weight, partner * width, width, 1)
        weight_pieces.append(piece if mask == 0 else xor_tp(piece, mask, n_tp))

    head_ids = tp_index * head_count + jnp.arange(head_count, dtype=jnp.int32)
    pair_ids = head_ids // (QH // KVH) - tp_index
    select = (pair_ids[:, None] == jnp.arange(2, dtype=jnp.int32)[None, :]).astype(jnp.bfloat16)
    req_lengths = lengths[0]
    req_tenant = tenant[0]
    req_ends = jnp.cumsum(req_lengths)
    req_starts = req_ends - req_lengths
    position = jnp.arange(row_count, dtype=jnp.int32)
    request_ids = jnp.sum((position[:, None] >= req_ends[None, :]).astype(jnp.int32), axis=1)
    member = request_ids[:, None] == jnp.arange(req_lengths.shape[0], dtype=jnp.int32)[None, :]
    row_start = jnp.sum(jnp.where(member, req_starts[None, :], 0), axis=1)
    row_tenant = jnp.sum(jnp.where(member, req_tenant[None, :], 0), axis=1)
    score_scale = HD ** (-0.5)
    own_slot = jnp.transpose(
        prefix_cache.reshape(prefix_cache.shape[0], 2, 2, HD), (0, 2, 1, 3)
    ).reshape(prefix_cache.shape[0], -1)
    slots, slot_of_tenant = tenant_slots(own_slot, owners, n_req)
    suffix_rows = jnp.transpose(suffix_kv.reshape(row_count, 2, 2, HD), (0, 2, 1, 3)).reshape(
        row_count, -1
    )
    window = min(MOSTLEN, row_count)
    firsts = jnp.minimum(req_starts, row_count - window).astype(jnp.int32)
    head_select = jnp.transpose(select)[:, :, None, None]
    spreads = []
    suffix_windows = []
    for request in range(req_lengths.shape[0]):
        window_queries = lax.dynamic_slice_in_dim(queries, firsts[request], window, 0)
        window_queries = jnp.transpose(window_queries.reshape(window, head_count, HD), (1, 0, 2))
        spread = jnp.concatenate(
            [window_queries * head_select[0], window_queries * head_select[1]], axis=2
        )
        spreads.append((spread * score_scale).reshape(head_count * window, 2 * HD))
        suffix_windows.append(lax.dynamic_slice_in_dim(suffix_rows, firsts[request], window, 0))
    query_rows = (jnp.arange(head_count * window, dtype=jnp.int32) % window)[:, None]
    row_pairs = jnp.repeat(pair_ids.astype(jnp.int32), window)[:, None]
    slot_index = slot_of_tenant[req_tenant].astype(jnp.int32)
    results = window_attention(
        slot_index,
        firsts,
        req_starts.astype(jnp.int32),
        jnp.stack(spreads),
        slots,
        jnp.stack(suffix_windows),
        query_rows,
        row_pairs,
        own_slot.shape[0],
    ).reshape(-1, head_count, window, HD)
    attended = jnp.zeros((row_count, head_count * HD), jnp.bfloat16)
    for request in range(req_lengths.shape[0]):
        window_attended = jnp.transpose(results[request], (1, 0, 2)).reshape(window, -1)
        placed = lax.dynamic_update_slice_in_dim(
            jnp.zeros_like(attended), window_attended, firsts[request], 0
        )
        attended = jnp.where((request_ids == request)[:, None], placed, attended)

    head_blocks = from_partners(attended, n_tp)
    projected = None
    for mask in range(n_tp):
        part = jnp.dot(head_blocks[mask], weight_pieces[mask], preferred_element_type=jnp.float32)
        projected = part if projected is None else projected + part
    new_residual = (residual.astype(jnp.float32) + projected).astype(jnp.bfloat16)

    blocks = from_partners(new_residual, n_tp)
    widened = [block.astype(jnp.float32) for block in blocks]
    square_sums = sum(jnp.sum(block * block, axis=1, keepdims=True) for block in widened)
    mean_square = square_sums / (width * n_tp)
    scale = lax.rsqrt(mean_square + 1e-05)
    gain = norm_gain.astype(jnp.float32)
    next_sums = None
    for mask in range(n_tp):
        source = tp_index ^ mask
        block_gain = lax.dynamic_slice_in_dim(gain, source * width, width, 0)
        block_weight = lax.dynamic_slice_in_dim(next_query_weight, source * width, width, 0)
        normed = (widened[mask] * scale * block_gain).astype(jnp.bfloat16)
        part = jnp.dot(normed, block_weight, preferred_element_type=jnp.float32)
        next_sums = part if next_sums is None else next_sums + part
    return (new_residual, next_sums.astype(jnp.bfloat16))


def solution(mesh):
    n_req = mesh.shape["req"]
    n_tp = mesh.shape["tp"]

    def body(*args):
        return local(*args, n_req=n_req, n_tp=n_tp)

    return jax.shard_map(
        body,
        mesh=mesh,
        in_specs=(
            P("req", "tp"),
            P("req", "tp"),
            P("req", "tp", None),
            P("req", "tp", None),
            P("tp", None),
            P(),
            P(None, "tp"),
            P("req", None),
            P("req", None),
            P(),
        ),
        out_specs=(P("req", "tp"), P("req", "tp")),
        check_vma=False,
    )
```

profile of v0, /device:TPU:8, one launch (start us, length us, event | category | flops | bytes accessed | tf_op | source)
XLA Modules:
  0.0 102.0 jit_solution(3614600891780798670)
XLA Ops:
  0.7 1.4 %copy.48 = bf16[1024,1,256]{0,2,1:T(8,128)(2,1)S(1)} copy(bf16[1024,1,256]{2,0,1:T(8,128)(2,1)} %param.13) | data formatting | bytes 1048576 | tf_op args[3]
  2.4 1.6 %collective-permute-start.1 = (bf16[1024,256]{1,0:T(8,128)(2,1)S(1)}, bf16[1024,256]{1,0:T(8,128)(2,1)}, u32[]{:S(2)}, u32[]{:S(2)}) collective-permute-start(bf16[1024,256]{1,0:T(8,128)(2,1)S(1)} %copy.54), channel_id=1, source_target_pairs={{0,8},{4,12},{8,0},{12,4},{16,24},{20,28},{24,16},{28,20},{1,9},{5... | collective-permute-start | bytes 1572872 | tf_op jit(solution)/shard_map/ppermute | solution.py:34
  3.9 1.5 %collective-permute-start.3 = (bf16[1024,256]{1,0:T(8,128)(2,1)S(1)}, bf16[1024,256]{1,0:T(8,128)(2,1)}, u32[]{:S(2)}, u32[]{:S(2)}) collective-permute-start(bf16[1024,256]{1,0:T(8,128)(2,1)S(1)} %copy.54), channel_id=1, source_target_pairs={{0,16},{4,20},{8,24},{12,28},{16,0},{20,4},{24,8},{28,12},{1,17},{... | collective-permute-start | bytes 1572872 | tf_op jit(solution)/shard_map/ppermute | solution.py:34
  5.5 0.5 collective-permute-start.5
  5.9 2.2 %constant_dynamic-slice_fusion = (bf16[320,512]{1,0:T(8,128)(2,1)}, bf16[320,512]{1,0:T(8,128)(2,1)}, bf16[320,512]{1,0:T(8,128)(2,1)}) fusion(bf16[320,2048]{1,0:T(8,128)(2,1)} %param.14, s32[]{:T(128)S(6)} %select_n.131, s32[]{:T(128)S(6)} %select_n.129, s32[]{:T(128)S(6)} %select_n.130), kind=kLoop, calls=%fused_computation.80 | loop fusion | bytes 1966092 | tf_op jit(solution)/shard_map/dynamic_slice | solution.py:162
  8.3 0.5 broadcast_minimum_fusion
  8.8 0.6 fusion.47
  17.7 0.8 add_select_fusion.row_ref
  20.4 1.0 %copy.55 = bf16[256,1,256]{0,2,1:T(8,128)(2,1)S(1)} copy(bf16[256,1,256]{2,0,1:T(8,128)(2,1)} %param.12) | data formatting | bytes 262144 | tf_op args[2]
  21.9 0.7 copy.58
  22.6 0.7 copy.57
  23.4 0.8 constant_dynamic-update-slice_fusion.7
  24.2 1.6 %pad_maximum_fusion.1.suffix_ref = bf16[4,128,256]{2,1,0:T(8,128)(2,1)} fusion(bf16[1,128,256]{2,1,0:T(8,128)(2,1)S(1)} %bitcast.114, bf16[1,128,256]{2,1,0:T(8,128)(2,1)S(1)} %bitcast.115, bf16[1,128,256]{2,1,0:T(8,128)(2,1)} %bitcast.116, bf16[1,128,256]{2,1,0:T(8,128)(2,1)} %bitcast.117), kind=kLoop, calls=%fused_computation.43 | loop fusion | flops 393216 | bytes 524288 | tf_op jit(solution)/shard_map/stack | solution.py:207
  25.8 0.9 pad_maximum_fusion.query_ref
  26.8 2.5 %collective-permute-done.3 = bf16[1024,256]{1,0:T(8,128)(2,1)} collective-permute-done((bf16[1024,256]{1,0:T(8,128)(2,1)S(1)}, bf16[1024,256]{1,0:T(8,128)(2,1)}, u32[]{:S(2)}, u32[]{:S(2)}) %collective-permute-start.3) | collective-permute-done | bytes 524320 | tf_op jit(solution)/shard_map/ppermute | solution.py:34
  29.3 0.9 copy.67
  30.3 1.1 %gather_fusion = s32[4]{0:T(128)} fusion(s32[4]{0:T(128)S(1)} %fusion.42, s32[1024]{0:T(1024)S(1)} %pad_clamp_fusion), kind=kCustom, calls=%fused_computation | custom fusion | bytes 48 | tf_op jit(solution)/shard_map/gather | solution.py:200
  31.5 2.6 %collective-permute-start.10 = (bf16[320,512]{1,0:T(8,128)(2,1)}, bf16[320,512]{1,0:T(8,128)(2,1)}, u32[]{:S(2)}, u32[]{:S(2)}) collective-permute-start(bf16[320,512]{1,0:T(8,128)(2,1)} %get-tuple-element.6), channel_id=1, source_target_pairs={{0,2},{1,3},{2,0},{3,1},{4,6},{5,7},{6,4},{7,5},{8,10},{9,11},{10,... | collective-permute-start | bytes 983048 | tf_op jit(solution)/shard_map/ppermute | solution.py:124
  34.3 1.9 %constant_dynamic-update-slice_fusion.6 = bf16[8192,256]{1,0:T(8,128)(2,1)} fusion(bf16[8192,256]{1,0:T(8,128)(2,1)} %constant_dynamic-update-slice_fusion.7, bf16[1024,256]{1,0:T(8,128)(2,1)} %collective-permute-done), kind=kLoop, calls=%fused_computation.72 | loop fusion | bytes 1048576
  36.1 1.9 %constant_dynamic-update-slice_fusion.5 = bf16[8192,256]{1,0:T(8,128)(2,1)} fusion(bf16[8192,256]{1,0:T(8,128)(2,1)} %constant_dynamic-update-slice_fusion.6, bf16[1024,256]{1,0:T(8,128)(2,1)} %collective-permute-done.1), kind=kLoop, calls=%fused_computation.71 | loop fusion | bytes 1048576
  38.0 0.9 constant_dynamic-update-slice_fusion.4
  38.9 1.9 %constant_dynamic-update-slice_fusion.3 = bf16[8192,256]{1,0:T(8,128)(2,1)} fusion(bf16[8192,256]{1,0:T(8,128)(2,1)} %constant_dynamic-update-slice_fusion.4, bf16[1024,256]{1,0:T(8,128)(2,1)} %collective-permute-done.3), kind=kLoop, calls=%fused_computation.69 | loop fusion | bytes 1048576
  40.7 0.8 constant_dynamic-update-slice_fusion.2
  41.6 1.9 %constant_dynamic-update-slice_fusion.1 = bf16[8192,256]{1,0:T(8,128)(2,1)} fusion(bf16[8192,256]{1,0:T(8,128)(2,1)} %constant_dynamic-update-slice_fusion.2, bf16[1024,256]{1,0:T(8,128)(2,1)} %collective-permute-done.5), kind=kLoop, calls=%fused_computation.67 | loop fusion | bytes 1048576
  43.4 0.8 constant_dynamic-update-slice_fusion.prefix_ref
  44.3 9.9 %shard_map.113 = bf16[4,640,64]{2,1,0:T(8,128)(2,1)} custom-call(s32[4]{0:T(128)} %gather_fusion, s32[4]{0:T(128)} %copy-done.5, s32[4]{0:T(128)} %get-tuple-element.3.start_ref, bf16[4,640,128]{2,1,0:T(8,128)(2,1)} %pad_maximum_fusion.query_ref, bf16[8192,256]{1,0:T(8,128)(2,1)} %constant_dynamic-update-slice_fusion.prefix_ref, ...), custom_call_target="tpu_custom_call" | custom-call | tf_op jit(solution)/shard_map/pallas_call | solution.py:115
  54.1 1.2 %fusion.45 = (bf16[1,640,64]{2,1,0:T(8,128)(2,1)S(1)}, bf16[1,640,64]{2,1,0:T(8,128)(2,1)S(1)}, bf16[1,640,64]{2,1,0:T(8,128)(2,1)S(1)}, bf16[1,640,64]{2,1,0:T(8,128)(2,1)S(1)}) fusion(bf16[4,640,64]{2,1,0:T(8,128)(2,1)} %shard_map.113), kind=kLoop, calls=%fused_computation.119 | loop fusion | bytes 655360 | tf_op jit(solution)/shard_map/slice | solution.py:214
  56.0 0.3 dynamic_update_slice.10
  56.3 0.3 dynamic_update_slice.11
  56.7 0.7 dynamic_update_slice.12
  57.4 0.4 select_n.124
  57.8 1.9 %collective-permute-start.7 = (bf16[256,320]{0,1:T(8,128)(2,1)S(1)}, bf16[256,320]{0,1:T(8,128)(2,1)S(1)}, u32[]{:S(2)}, u32[]{:S(2)}) collective-permute-start(bf16[256,320]{0,1:T(8,128)(2,1)S(1)} %select_select_fusion), channel_id=1, source_target_pairs={{0,1},{1,0},{2,3},{3,2},{4,5},{5,4},{6,7},{7,6},{8,9},{9,8},{10,11... | collective-permute-start | bytes 491528 | tf_op jit(solution)/shard_map/ppermute | solution.py:124
  59.7 1.7 %collective-permute-start.9 = (bf16[256,320]{0,1:T(8,128)(2,1)S(1)}, bf16[256,320]{0,1:T(8,128)(2,1)S(1)}, u32[]{:S(2)}, u32[]{:S(2)}) collective-permute-start(bf16[256,320]{0,1:T(8,128)(2,1)S(1)} %select_select_fusion), channel_id=1, source_target_pairs={{0,2},{1,3},{2,0},{3,1},{4,6},{5,7},{6,4},{7,5},{8,10},{9,11},{10,... | collective-permute-start | bytes 491528 | tf_op jit(solution)/shard_map/ppermute | solution.py:124
  61.4 1.3 %fusion.20 = f32[256,512]{1,0:T(8,128)S(1)} fusion(bf16[256,320]{0,1:T(8,128)(2,1)S(1)} %select_select_fusion, bf16[320,2048]{1,0:T(8,128)(2,1)} %param.14, s32[]{:T(128)S(6)} %select_n.128), kind=kOutput, calls=%fused_computation.37 | convolution fusion | flops 83886080 | bytes 1015812 | tf_op jit(solution)/shard_map/dot_general | solution.py:223
  62.7 7.2 %collective-permute-done.9 = bf16[256,320]{0,1:T(8,128)(2,1)S(1)} collective-permute-done((bf16[256,320]{0,1:T(8,128)(2,1)S(1)}, bf16[256,320]{0,1:T(8,128)(2,1)S(1)}, u32[]{:S(2)}, u32[]{:S(2)}) %collective-permute-start.9) | collective-permute-done | bytes 163872 | tf_op jit(solution)/shard_map/ppermute | solution.py:124
  69.9 1.4 %collective-permute-start.11 = (bf16[256,320]{0,1:T(8,128)(2,1)S(1)}, bf16[256,320]{0,1:T(8,128)(2,1)S(1)}, u32[]{:S(2)}, u32[]{:S(2)}) collective-permute-start(bf16[256,320]{0,1:T(8,128)(2,1)S(1)} %collective-permute-done.9), channel_id=1, source_target_pairs={{0,1},{1,0},{2,3},{3,2},{4,5},{5,4},{6,7},{7,6},{8,9},{9,8},{10,11... | collective-permute-start | bytes 491528 | tf_op jit(solution)/shard_map/ppermute | solution.py:124
  71.3 1.3 %convolution_add_fusion.2 = f32[256,512]{1,0:T(8,128)S(1)} fusion(f32[256,512]{1,0:T(8,128)S(1)} %fusion.20, bf16[256,320]{0,1:T(8,128)(2,1)S(1)} %collective-permute-done.7, bf16[320,512]{1,0:T(8,128)(2,1)} %collective-permute-done.8), kind=kOutput, calls=%fused_computation.4 | convolution fusion | flops 84017152 | bytes 1540096 | tf_op jit(solution)/shard_map/dot_general | solution.py:223
  72.6 1.3 %convolution_add_fusion.1 = f32[256,512]{1,0:T(8,128)S(1)} fusion(f32[256,512]{1,0:T(8,128)S(1)} %convolution_add_fusion.2, bf16[256,320]{0,1:T(8,128)(2,1)S(1)} %collective-permute-done.9, bf16[320,512]{1,0:T(8,128)(2,1)} %collective-permute-done.10), kind=kOutput, calls=%fused_computation.3 | convolution fusion | flops 84017152 | bytes 1540096 | tf_op jit(solution)/shard_map/dot_general | solution.py:223
  73.9 2.1 %collective-permute-done.11 = bf16[256,320]{0,1:T(8,128)(2,1)S(1)} collective-permute-done((bf16[256,320]{0,1:T(8,128)(2,1)S(1)}, bf16[256,320]{0,1:T(8,128)(2,1)S(1)}, u32[]{:S(2)}, u32[]{:S(2)}) %collective-permute-start.11) | collective-permute-done | bytes 163872 | tf_op jit(solution)/shard_map/ppermute | solution.py:124
  76.0 1.4 %fusion.3 = (f32[256]{0:T(256)S(1)}, bf16[256,512]{1,0:T(8,128)(2,1)S(1)}) fusion(f32[256,512]{1,0:T(8,128)S(1)} %convolution_add_fusion.1, bf16[256,320]{0,1:T(8,128)(2,1)S(1)} %collective-permute-done.11, bf16[320,512]{1,0:T(8,128)(2,1)} %collective-permute-done.12, bf16[256,512]{1,0:T(8,128)(2,1)S(1)} %copy-done.4), kind=kOutput, calls=%fused_computation.19 | convolution fusion | flops 84803328 | bytes 1541120 | tf_op jit(solution)/shard_map/dot_general | solution.py:223
  77.5 3.4 %collective-permute-start.14 = (bf16[256,512]{1,0:T(8,128)(2,1)S(1)}, bf16[256,512]{1,0:T(8,128)(2,1)S(1)}, u32[]{:S(2)}, u32[]{:S(2)}) collective-permute-start(bf16[256,512]{1,0:T(8,128)(2,1)S(1)} %get-tuple-element.48), channel_id=1, source_target_pairs={{0,2},{1,3},{2,0},{3,1},{4,6},{5,7},{6,4},{7,5},{8,10},{9,11},{10,... | collective-permute-start | bytes 786440 | tf_op jit(solution)/shard_map/ppermute | solution.py:124
  81.2 10.3 %collective-permute-done.14 = bf16[256,512]{1,0:T(8,128)(2,1)S(1)} collective-permute-done((bf16[256,512]{1,0:T(8,128)(2,1)S(1)}, bf16[256,512]{1,0:T(8,128)(2,1)S(1)}, u32[]{:S(2)}, u32[]{:S(2)}) %collective-permute-start.14) | collective-permute-done | bytes 262176 | tf_op jit(solution)/shard_map/ppermute | solution.py:124
  91.5 1.4 %collective-permute-start.15 = (bf16[256,512]{1,0:T(8,128)(2,1)S(1)}, bf16[256,512]{1,0:T(8,128)(2,1)S(1)}, u32[]{:S(2)}, u32[]{:S(2)}) collective-permute-start(bf16[256,512]{1,0:T(8,128)(2,1)S(1)} %collective-permute-done.14), channel_id=1, source_target_pairs={{0,1},{1,0},{2,3},{3,2},{4,5},{5,4},{6,7},{7,6},{8,9},{9,8},{10,11... | collective-permute-start | bytes 786440 | tf_op jit(solution)/shard_map/ppermute | solution.py:124
  93.3 6.4 %collective-permute-done.15 = bf16[256,512]{1,0:T(8,128)(2,1)S(1)} collective-permute-done((bf16[256,512]{1,0:T(8,128)(2,1)S(1)}, bf16[256,512]{1,0:T(8,128)(2,1)S(1)}, u32[]{:S(2)}, u32[]{:S(2)}) %collective-permute-start.15) | collective-permute-done | bytes 262176 | tf_op jit(solution)/shard_map/ppermute | solution.py:124
  99.8 0.4 fusion.18
  100.2 0.4 convolution_add_fusion.5
  100.6 0.4 convolution_add_fusion.4
  100.9 1.0 %fusion.2 = bf16[256,320]{0,1:T(8,128)(2,1)} fusion(f32[256,320]{0,1:T(8,128)S(1)} %convolution_add_fusion.4, bf16[2048,320]{0,1:T(8,128)(2,1)S(1)} %copy-done, s32[]{:T(128)S(6)} %select_n.131, bf16[256,512]{1,0:T(8,128)(2,1)S(1)} %collective-permute-done.15, f32[512]{0:T(512)S(1)} %get-tuple-element.27, f32[256]{0:T(256)S(1)} %add_rsqrt_fusion), kind=kOutput, calls=%fused_computation.9 | convolution fusion | flops 84574208 | bytes 1084420 | tf_op jit(solution)/shard_map/dot_general | solution.py:239
  (83 shorter events, 5.1 us)
Async XLA Ops:
  0.6 99.2 %copy-start = (bf16[2048,320]{0,1:T(8,128)(2,1)S(1)}, bf16[2048,320]{0,1:T(8,128)(2,1)}, u32[]{:S(2)}) copy-start(bf16[2048,320]{0,1:T(8,128)(2,1)} %param.16) | copy-start | bytes 3932164
  0.6 7.5 %copy-start.7 = (s32[1,4]{1,0:T(1,128)S(1)}, s32[1,4]{1,0:T(1,128)}, u32[]{:S(2)}) copy-start(s32[1,4]{1,0:T(1,128)} %param.17) | copy-start | bytes 52
  0.7 14.0 %copy-start.9 = (s32[1,4]{1,0:T(1,128)S(1)}, s32[1,4]{1,0:T(1,128)}, u32[]{:S(2)}) copy-start(s32[1,4]{1,0:T(1,128)} %param.18) | copy-start | bytes 52
  0.7 16.7 %copy-start.8 = (s32[4]{0:T(128)S(1)}, s32[4]{0:T(128)}, u32[]{:S(2)}) copy-start(s32[4]{0:T(128)} %param.19) | copy-start | bytes 52
  0.7 16.7 %copy-start.2 = (bf16[256,320]{0,1:T(8,128)(2,1)S(1)}, bf16[256,320]{0,1:T(8,128)(2,1)}, u32[]{:S(2)}) copy-start(bf16[256,320]{0,1:T(8,128)(2,1)} %param.11) | copy-start | bytes 491524
  2.3 29.2 %collective-permute-start = (bf16[1024,256]{1,0:T(8,128)(2,1)S(1)}, bf16[1024,256]{1,0:T(8,128)(2,1)}, u32[]{:S(2)}, u32[]{:S(2)}) collective-permute-start(bf16[1024,256]{1,0:T(8,128)(2,1)S(1)} %copy.54), channel_id=1, source_target_pairs={{0,4},{4,0},{8,12},{12,8},{16,20},{20,16},{24,28},{28,24},{1,5},{5... | collective-permute-start | bytes 1572872 | tf_op jit(solution)/shard_map/ppermute | solution.py:34
  2.4 21.8 %collective-permute-start.1 = (bf16[1024,256]{1,0:T(8,128)(2,1)S(1)}, bf16[1024,256]{1,0:T(8,128)(2,1)}, u32[]{:S(2)}, u32[]{:S(2)}) collective-permute-start(bf16[1024,256]{1,0:T(8,128)(2,1)S(1)} %copy.54), channel_id=1, source_target_pairs={{0,8},{4,12},{8,0},{12,4},{16,24},{20,28},{24,16},{28,20},{1,9},{5... | collective-permute-start | bytes 1572872 | tf_op jit(solution)/shard_map/ppermute | solution.py:34
  3.9 25.3 %collective-permute-start.3 = (bf16[1024,256]{1,0:T(8,128)(2,1)S(1)}, bf16[1024,256]{1,0:T(8,128)(2,1)}, u32[]{:S(2)}, u32[]{:S(2)}) collective-permute-start(bf16[1024,256]{1,0:T(8,128)(2,1)S(1)} %copy.54), channel_id=1, source_target_pairs={{0,16},{4,20},{8,24},{12,28},{16,0},{20,4},{24,8},{28,12},{1,17},{... | collective-permute-start | bytes 1572872 | tf_op jit(solution)/shard_map/ppermute | solution.py:34
  5.5 28.6 %collective-permute-start.5 = (bf16[1024,256]{1,0:T(8,128)(2,1)S(1)}, bf16[1024,256]{1,0:T(8,128)(2,1)}, u32[]{:S(2)}, u32[]{:S(2)}) collective-permute-start(bf16[1024,256]{1,0:T(8,128)(2,1)S(1)} %copy.54), channel_id=1, source_target_pairs={{0,24},{4,28},{8,16},{12,20},{16,8},{20,12},{24,0},{28,4},{1,25},{... | collective-permute-start | bytes 1572872 | tf_op jit(solution)/shard_map/ppermute | solution.py:34
  8.1 63.2 %collective-permute-start.8 = (bf16[320,512]{1,0:T(8,128)(2,1)}, bf16[320,512]{1,0:T(8,128)(2,1)}, u32[]{:S(2)}, u32[]{:S(2)}) collective-permute-start(bf16[320,512]{1,0:T(8,128)(2,1)} %get-tuple-element.5), channel_id=1, source_target_pairs={{0,1},{1,0},{2,3},{3,2},{4,5},{5,4},{6,7},{7,6},{8,9},{9,8},{10,11... | collective-permute-start | bytes 983048 | tf_op jit(solution)/shard_map/ppermute | solution.py:124
  8.8 15.4 %copy-start.5 = (s32[4]{0:T(128)}, s32[4]{0:T(128)S(1)}, u32[]{:S(2)}) copy-start(s32[4]{0:T(128)S(1)} %get-tuple-element.2.first_ref) | copy-start | bytes 52
  20.4 17.6 %copy-start.3 = (bf16[320,512]{1,0:T(8,128)(2,1)S(1)}, bf16[320,512]{1,0:T(8,128)(2,1)}, u32[]{:S(2)}) copy-start(bf16[320,512]{1,0:T(8,128)(2,1)} %get-tuple-element.4) | copy-start | bytes 983044
  24.2 13.8 %collective-permute-start.2 = (bf16[1024,256]{1,0:T(8,128)(2,1)}, bf16[1024,256]{1,0:T(8,128)(2,1)S(1)}, u32[]{:S(2)}, u32[]{:S(2)}) collective-permute-start(bf16[1024,256]{1,0:T(8,128)(2,1)} %collective-permute-done.1), channel_id=1, source_target_pairs={{0,4},{4,0},{8,12},{12,8},{16,20},{20,16},{24,28},{28,24},{1,5},{5... | collective-permute-start | bytes 1572872 | tf_op jit(solution)/shard_map/ppermute | solution.py:34
  29.3 11.5 %collective-permute-start.4 = (bf16[1024,256]{1,0:T(8,128)(2,1)}, bf16[1024,256]{1,0:T(8,128)(2,1)S(1)}, u32[]{:S(2)}, u32[]{:S(2)}) collective-permute-start(bf16[1024,256]{1,0:T(8,128)(2,1)} %collective-permute-done.3), channel_id=1, source_target_pairs={{0,4},{4,0},{8,12},{12,8},{16,20},{20,16},{24,28},{28,24},{1,5},{5... | collective-permute-start | bytes 1572872 | tf_op jit(solution)/shard_map/ppermute | solution.py:34
  31.5 41.1 %collective-permute-start.10 = (bf16[320,512]{1,0:T(8,128)(2,1)}, bf16[320,512]{1,0:T(8,128)(2,1)}, u32[]{:S(2)}, u32[]{:S(2)}) collective-permute-start(bf16[320,512]{1,0:T(8,128)(2,1)} %get-tuple-element.6), channel_id=1, source_target_pairs={{0,2},{1,3},{2,0},{3,1},{4,6},{5,7},{6,4},{7,5},{8,10},{9,11},{10,... | collective-permute-start | bytes 983048 | tf_op jit(solution)/shard_map/ppermute | solution.py:124
  34.0 9.4 %collective-permute-start.6 = (bf16[1024,256]{1,0:T(8,128)(2,1)}, bf16[1024,256]{1,0:T(8,128)(2,1)S(1)}, u32[]{:S(2)}, u32[]{:S(2)}) collective-permute-start(bf16[1024,256]{1,0:T(8,128)(2,1)} %collective-permute-done.5), channel_id=1, source_target_pairs={{0,4},{4,0},{8,12},{12,8},{16,20},{20,16},{24,28},{28,24},{1,5},{5... | collective-permute-start | bytes 1572872 | tf_op jit(solution)/shard_map/ppermute | solution.py:34
  38.0 35.9 %collective-permute-start.12 = (bf16[320,512]{1,0:T(8,128)(2,1)S(1)}, bf16[320,512]{1,0:T(8,128)(2,1)}, u32[]{:S(2)}, u32[]{:S(2)}) collective-permute-start(bf16[320,512]{1,0:T(8,128)(2,1)S(1)} %copy-done.3), channel_id=1, source_target_pairs={{0,3},{1,2},{2,1},{3,0},{4,7},{5,6},{6,5},{7,4},{8,11},{9,10},{10,... | collective-permute-start | bytes 983048 | tf_op jit(solution)/shard_map/ppermute | solution.py:124
  54.1 21.9 %copy-start.4 = (bf16[256,512]{1,0:T(8,128)(2,1)S(1)}, bf16[256,512]{1,0:T(8,128)(2,1)}, u32[]{:S(2)}) copy-start(bf16[256,512]{1,0:T(8,128)(2,1)} %param.10) | copy-start | bytes 786436
  55.7 37.3 %copy-start.6 = (bf16[2048]{0:T(1024)(128)(2,1)S(1)}, bf16[2048]{0:T(1024)(128)(2,1)}, u32[]{:S(2)}) copy-start(bf16[2048]{0:T(1024)(128)(2,1)} %param.15) | copy-start | bytes 12292
  57.8 13.4 %collective-permute-start.7 = (bf16[256,320]{0,1:T(8,128)(2,1)S(1)}, bf16[256,320]{0,1:T(8,128)(2,1)S(1)}, u32[]{:S(2)}, u32[]{:S(2)}) collective-permute-start(bf16[256,320]{0,1:T(8,128)(2,1)S(1)} %select_select_fusion), channel_id=1, source_target_pairs={{0,1},{1,0},{2,3},{3,2},{4,5},{5,4},{6,7},{7,6},{8,9},{9,8},{10,11... | collective-permute-start | bytes 491528 | tf_op jit(solution)/shard_map/ppermute | solution.py:124
  59.7 10.2 %collective-permute-start.9 = (bf16[256,320]{0,1:T(8,128)(2,1)S(1)}, bf16[256,320]{0,1:T(8,128)(2,1)S(1)}, u32[]{:S(2)}, u32[]{:S(2)}) collective-permute-start(bf16[256,320]{0,1:T(8,128)(2,1)S(1)} %select_select_fusion), channel_id=1, source_target_pairs={{0,2},{1,3},{2,0},{3,1},{4,6},{5,7},{6,4},{7,5},{8,10},{9,11},{10,... | collective-permute-start | bytes 491528 | tf_op jit(solution)/shard_map/ppermute | solution.py:124
  69.9 6.2 %collective-permute-start.11 = (bf16[256,320]{0,1:T(8,128)(2,1)S(1)}, bf16[256,320]{0,1:T(8,128)(2,1)S(1)}, u32[]{:S(2)}, u32[]{:S(2)}) collective-permute-start(bf16[256,320]{0,1:T(8,128)(2,1)S(1)} %collective-permute-done.9), channel_id=1, source_target_pairs={{0,1},{1,0},{2,3},{3,2},{4,5},{5,4},{6,7},{7,6},{8,9},{9,8},{10,11... | collective-permute-start | bytes 491528 | tf_op jit(solution)/shard_map/ppermute | solution.py:124
  77.4 24.5 %copy-start.1 = (bf16[256,512]{1,0:T(8,128)(2,1)}, bf16[256,512]{1,0:T(8,128)(2,1)S(1)}, u32[]{:S(2)}) copy-start(bf16[256,512]{1,0:T(8,128)(2,1)S(1)} %get-tuple-element.48) | copy-start | bytes 786436
  77.5 14.0 %collective-permute-start.14 = (bf16[256,512]{1,0:T(8,128)(2,1)S(1)}, bf16[256,512]{1,0:T(8,128)(2,1)S(1)}, u32[]{:S(2)}, u32[]{:S(2)}) collective-permute-start(bf16[256,512]{1,0:T(8,128)(2,1)S(1)} %get-tuple-element.48), channel_id=1, source_target_pairs={{0,2},{1,3},{2,0},{3,1},{4,6},{5,7},{6,4},{7,5},{8,10},{9,11},{10,... | collective-permute-start | bytes 786440 | tf_op jit(solution)/shard_map/ppermute | solution.py:124
  80.9 12.2 %collective-permute-start.13 = (bf16[256,512]{1,0:T(8,128)(2,1)S(1)}, bf16[256,512]{1,0:T(8,128)(2,1)S(1)}, u32[]{:S(2)}, u32[]{:S(2)}) collective-permute-start(bf16[256,512]{1,0:T(8,128)(2,1)S(1)} %get-tuple-element.48), channel_id=1, source_target_pairs={{0,1},{1,0},{2,3},{3,2},{4,5},{5,4},{6,7},{7,6},{8,9},{9,8},{10,11... | collective-permute-start | bytes 786440 | tf_op jit(solution)/shard_map/ppermute | solution.py:124
  91.5 8.2 %collective-permute-start.15 = (bf16[256,512]{1,0:T(8,128)(2,1)S(1)}, bf16[256,512]{1,0:T(8,128)(2,1)S(1)}, u32[]{:S(2)}, u32[]{:S(2)}) collective-permute-start(bf16[256,512]{1,0:T(8,128)(2,1)S(1)} %collective-permute-done.14), channel_id=1, source_target_pairs={{0,1},{1,0},{2,3},{3,2},{4,5},{5,4},{6,7},{7,6},{8,9},{9,8},{10,11... | collective-permute-start | bytes 786440 | tf_op jit(solution)/shard_map/ppermute | solution.py:124
where the time goes:
time: 104 us; the launch traced here: 102 us
  waiting for transfers between devices  28.6 us (28%)
  local copies, waits for them, and re-layouts  25.7 us (25%)
  starting transfers between devices  16.5 us (16%)
  Pallas kernels  9.89 us (10%)
  between operations  8.72 us (8%)
  matrix products  7.38 us (7%)
  other arithmetic  5.15 us (5%)
    ppermute x9, waiting for transfers between devices, xor_tp(): return lax.ppermute(block, 'tp', pairs)  26.1 us
    unnamed x32, local copies, waits for them, and re-layouts  13.4 us
    ppermute x9, starting transfers between devices, xor_tp(): return lax.ppermute(block, 'tp', pairs)  12.7 us
    pallas_call x1, Pallas kernels, window_attention(): pl.pallas_call(attention_kernel, grid_spec=grid_spec, out_shape=jax.Shape...  9.89 us
    dot_general x4, matrix products, local(): jnp.dot(head_blocks[mask], weight_pieces[mask], preferred_element_type=jn...  5.27 us
    ppermute x7, starting transfers between devices, xor_permute(): return lax.ppermute(block, 'req', pairs)  3.85 us
    ppermute x7, waiting for transfers between devices, xor_permute(): return lax.ppermute(block, 'req', pairs)  2.52 us
    dynamic_slice x1, local copies, waits for them, and re-layouts, local(): piece = lax.dynamic_slice_in_dim(out_weight, partner * width, width, 1)  2.16 us
  transfers between devices with their start and end apart: 16, of which 5 were waited for; matrix products, arithmetic and copies ran while one was open for 32% of the time, Pallas kernels for 10%

commit v1 on v0

--- a/solution.py
+++ b/solution.py
@@ -210,12 +210,15 @@
         own_slot.shape[0],
     ).reshape(-1, head_count, window, HD)
     attended = jnp.zeros((row_count, head_count * HD), jnp.bfloat16)
+    window_offsets = jnp.arange(window, dtype=jnp.int32)
     for request in range(req_lengths.shape[0]):
         window_attended = jnp.transpose(results[request], (1, 0, 2)).reshape(window, -1)
-        placed = lax.dynamic_update_slice_in_dim(
-            jnp.zeros_like(attended), window_attended, firsts[request], 0
+        window_rows = firsts[request] + window_offsets
+        mine = (window_rows >= req_starts[request]) & (window_rows < req_ends[request])
+        kept = lax.dynamic_slice_in_dim(attended, firsts[request], window, 0)
+        attended = lax.dynamic_update_slice_in_dim(
+            attended, jnp.where(mine[:, None], window_attended, kept), firsts[request], 0
         )
-        attended = jnp.where((request_ids == request)[:, None], placed, attended)
 
     head_blocks = from_partners(attended, n_tp)
     projected = None

time: 104 us -> 117 us (1.12)
  the two profiles are of different devices: /device:TPU:8 before, /device:TPU:0 now
where the time goes in v1:
time: 117 us; the launch traced here: 115 us
  local copies, waits for them, and re-layouts  30.9 us (26%)
  waiting for transfers between devices  26.1 us (22%)
  starting transfers between devices  18.9 us (16%)
  other arithmetic  13.9 us (12%)
  Pallas kernels  10.2 us (9%)
  between operations  8.24 us (7%)
  matrix products  6.4 us (5%)
    ppermute x9, waiting for transfers between devices, xor_tp(): return lax.ppermute(block, 'tp', pairs)  26.1 us
    ppermute x9, starting transfers between devices, xor_tp(): return lax.ppermute(block, 'tp', pairs)  13.7 us
    unnamed x36, local copies, waits for them, and re-layouts  13.4 us
    pallas_call x1, Pallas kernels, window_attention(): pl.pallas_call(attention_kernel, grid_spec=grid_spec, out_shape=jax.Shape...  10.2 us
    and x4, other arithmetic, local(): (window_rows >= req_starts[request]) & (window_rows < req_ends[request])  8.36 us
    dynamic_slice x5, local copies, waits for them, and re-layouts, local(): lax.dynamic_slice_in_dim(suffix_rows, firsts[request], window, 0)  6.56 us
    ppermute x7, starting transfers between devices, xor_permute(): return lax.ppermute(block, 'req', pairs)  5.19 us
    dot_general x4, matrix products, local(): jnp.dot(head_blocks[mask], weight_pieces[mask], preferred_element_type=jn...  4.3 us
  transfers between devices with their start and end apart: 16, of which 4 were waited for; matrix products, arithmetic and copies ran while one was open for 40% of the time, Pallas kernels for 9%

profile of v1, /device:TPU:0, one launch (start us, length us, event | category | flops | bytes accessed | tf_op | source)
XLA Modules:
  0.0 114.6 jit_solution(847006367539309209)
XLA Ops:
  0.7 1.4 %copy.22 = bf16[1024,1,256]{0,2,1:T(8,128)(2,1)S(1)} copy(bf16[1024,1,256]{2,0,1:T(8,128)(2,1)} %param.13) | data formatting | bytes 1048576 | tf_op args[3]
  2.8 2.6 %collective-permute-start.1 = (bf16[1024,256]{1,0:T(8,128)(2,1)S(1)}, bf16[1024,256]{1,0:T(8,128)(2,1)}, u32[]{:S(2)}, u32[]{:S(2)}) collective-permute-start(bf16[1024,256]{1,0:T(8,128)(2,1)S(1)} %copy.28), channel_id=1, source_target_pairs={{0,8},{4,12},{8,0},{12,4},{16,24},{20,28},{24,16},{28,20},{1,9},{5... | collective-permute-start | bytes 1572872 | tf_op jit(solution)/shard_map/ppermute | solution.py:34
  5.4 1.5 %collective-permute-start.3 = (bf16[1024,256]{1,0:T(8,128)(2,1)S(1)}, bf16[1024,256]{1,0:T(8,128)(2,1)}, u32[]{:S(2)}, u32[]{:S(2)}) collective-permute-start(bf16[1024,256]{1,0:T(8,128)(2,1)S(1)} %copy.28), channel_id=1, source_target_pairs={{0,16},{4,20},{8,24},{12,28},{16,0},{20,4},{24,8},{28,12},{1,17},{... | collective-permute-start | bytes 1572872 | tf_op jit(solution)/shard_map/ppermute | solution.py:34
  6.9 2.1 %constant_dynamic-slice_fusion = (bf16[320,512]{1,0:T(8,128)(2,1)}, bf16[320,512]{1,0:T(8,128)(2,1)}, bf16[320,512]{1,0:T(8,128)(2,1)}) fusion(bf16[320,2048]{1,0:T(8,128)(2,1)} %param.14, s32[]{:T(128)S(6)} %select_n.128, s32[]{:T(128)S(6)} %select_n.126, s32[]{:T(128)S(6)} %select_n.127), kind=kLoop, calls=%fused_computation.80 | loop fusion | bytes 1966092 | tf_op jit(solution)/shard_map/dynamic_slice | solution.py:162
  9.1 2.0 %collective-permute-start.8 = (bf16[320,512]{1,0:T(8,128)(2,1)}, bf16[320,512]{1,0:T(8,128)(2,1)}, u32[]{:S(2)}, u32[]{:S(2)}) collective-permute-start(bf16[320,512]{1,0:T(8,128)(2,1)} %get-tuple-element.5), channel_id=1, source_target_pairs={{0,1},{1,0},{2,3},{3,2},{4,5},{5,4},{6,7},{7,6},{8,9},{9,8},{10,11... | collective-permute-start | bytes 983048 | tf_op jit(solution)/shard_map/ppermute | solution.py:124
  11.3 0.7 fusion.47
  16.8 0.8 add_select_fusion.row_ref
  17.6 0.7 fusion.48
  22.5 1.0 copy.29
  23.5 0.9 constant_dynamic-slice_fusion.6
  24.4 1.0 copy.34
  25.4 1.6 %copy.33 = bf16[128,256]{1,0:T(8,128)(2,1)} copy(bf16[128,256]{0,1:T(8,128)(2,1)} %get-tuple-element.17) | data formatting | bytes 131072 | tf_op jit(solution)/shard_map/dynamic_slice | solution.py:197
  26.9 1.6 %copy.32 = bf16[128,256]{1,0:T(8,128)(2,1)} copy(bf16[128,256]{0,1:T(8,128)(2,1)} %get-tuple-element.18) | data formatting | bytes 131072 | tf_op jit(solution)/shard_map/dynamic_slice | solution.py:197
  28.5 1.6 %copy.31 = bf16[128,256]{1,0:T(8,128)(2,1)} copy(bf16[128,256]{0,1:T(8,128)(2,1)} %get-tuple-element.15) | data formatting | bytes 131072 | tf_op jit(solution)/shard_map/dynamic_slice | solution.py:197
  30.6 1.6 %pad_maximum_fusion.1.suffix_ref = bf16[4,128,256]{2,1,0:T(8,128)(2,1)} fusion(bf16[1,128,256]{2,1,0:T(8,128)(2,1)S(1)} %bitcast.122, bf16[1,128,256]{2,1,0:T(8,128)(2,1)} %bitcast.123, bf16[1,128,256]{2,1,0:T(8,128)(2,1)} %bitcast.124, bf16[1,128,256]{2,1,0:T(8,128)(2,1)} %bitcast.125), kind=kLoop, calls=%fused_computation.43 | loop fusion | flops 393216 | bytes 524288 | tf_op jit(solution)/shard_map/stack | solution.py:207
  32.2 0.7 fusion.42
  32.9 2.4 %compare_and_fusion.3 = pred[128]{0:T(512)(128)(4,1)} fusion(s32[]{:T(128)} %bitcast.5, s32[]{:T(128)} %bitcast.4, s32[]{:T(128)} %bitcast.3), kind=kLoop, calls=%fused_computation.104 | loop fusion | flops 512 | bytes 140 | tf_op jit(solution)/shard_map/and | solution.py:217
  35.3 2.3 %compare_and_fusion.2 = pred[128]{0:T(512)(128)(4,1)} fusion(s32[]{:T(128)} %bitcast.47, s32[]{:T(128)} %bitcast.46, s32[]{:T(128)} %bitcast.15), kind=kLoop, calls=%fused_computation.98 | loop fusion | flops 512 | bytes 140 | tf_op jit(solution)/shard_map/and | solution.py:217
  37.6 0.8 constant_dynamic-update-slice_fusion.7
  38.6 1.9 %compare_and_fusion.1 = pred[128]{0:T(512)(128)(4,1)S(1)} fusion(s32[]{:T(128)} %bitcast.52, s32[]{:T(128)} %bitcast.51, s32[]{:T(128)} %bitcast.21), kind=kLoop, calls=%fused_computation.97 | loop fusion | flops 512 | bytes 140 | tf_op jit(solution)/shard_map/and | solution.py:217
  40.4 0.9 pad_maximum_fusion.query_ref
  41.9 1.7 %compare_and_fusion = pred[128]{0:T(512)(128)(4,1)S(1)} fusion(s32[]{:T(128)} %bitcast.57, s32[]{:T(128)} %bitcast.56, s32[]{:T(128)} %bitcast.27), kind=kLoop, calls=%fused_computation.96 | loop fusion | flops 512 | bytes 140 | tf_op jit(solution)/shard_map/and | solution.py:217
  43.6 0.9 copy.41
  44.6 1.1 gather_fusion
  45.7 2.6 %collective-permute-start.10 = (bf16[320,512]{1,0:T(8,128)(2,1)}, bf16[320,512]{1,0:T(8,128)(2,1)S(1)}, u32[]{:S(2)}, u32[]{:S(2)}) collective-permute-start(bf16[320,512]{1,0:T(8,128)(2,1)} %get-tuple-element.6), channel_id=1, source_target_pairs={{0,2},{1,3},{2,0},{3,1},{4,6},{5,7},{6,4},{7,5},{8,10},{9,11},{10,... | collective-permute-start | bytes 983048 | tf_op jit(solution)/shard_map/ppermute | solution.py:124
  48.3 1.9 %constant_dynamic-update-slice_fusion.6 = bf16[8192,256]{1,0:T(8,128)(2,1)} fusion(bf16[8192,256]{1,0:T(8,128)(2,1)} %constant_dynamic-update-slice_fusion.7, bf16[1024,256]{1,0:T(8,128)(2,1)} %collective-permute-done), kind=kLoop, calls=%fused_computation.74 | loop fusion | bytes 1048576
  50.2 1.9 %constant_dynamic-update-slice_fusion.5 = bf16[8192,256]{1,0:T(8,128)(2,1)} fusion(bf16[8192,256]{1,0:T(8,128)(2,1)} %constant_dynamic-update-slice_fusion.6, bf16[1024,256]{1,0:T(8,128)(2,1)} %collective-permute-done.1), kind=kLoop, calls=%fused_computation.73 | loop fusion | bytes 1048576
  52.1 0.8 constant_dynamic-update-slice_fusion.4
  52.9 1.9 %constant_dynamic-update-slice_fusion.3 = bf16[8192,256]{1,0:T(8,128)(2,1)} fusion(bf16[8192,256]{1,0:T(8,128)(2,1)} %constant_dynamic-update-slice_fusion.4, bf16[1024,256]{1,0:T(8,128)(2,1)} %collective-permute-done.3), kind=kLoop, calls=%fused_computation.71 | loop fusion | bytes 1048576
  54.8 0.8 constant_dynamic-update-slice_fusion.2
  55.6 1.9 %constant_dynamic-update-slice_fusion.1 = bf16[8192,256]{1,0:T(8,128)(2,1)} fusion(bf16[8192,256]{1,0:T(8,128)(2,1)} %constant_dynamic-update-slice_fusion.2, bf16[1024,256]{1,0:T(8,128)(2,1)} %collective-permute-done.5), kind=kLoop, calls=%fused_computation.69 | loop fusion | bytes 1048576
  57.5 0.8 constant_dynamic-update-slice_fusion.prefix_ref
  58.3 10.2 %shard_map.113 = bf16[4,640,64]{2,1,0:T(8,128)(2,1)} custom-call(s32[4]{0:T(128)} %gather_fusion, s32[4]{0:T(128)} %copy-done.5, s32[4]{0:T(128)} %copy-done.6, bf16[4,640,128]{2,1,0:T(8,128)(2,1)} %pad_maximum_fusion.query_ref, bf16[8192,256]{1,0:T(8,128)(2,1)} %constant_dynamic-update-slice_fusion.prefix_ref, ...), custom_call_target="tpu_custom_call" | custom-call | tf_op jit(solution)/shard_map/pallas_call | solution.py:115
  68.5 1.2 %fusion.45 = (bf16[1,640,64]{2,1,0:T(8,128)(2,1)S(1)}, bf16[1,640,64]{2,1,0:T(8,128)(2,1)S(1)}, bf16[1,640,64]{2,1,0:T(8,128)(2,1)S(1)}, bf16[1,640,64]{2,1,0:T(8,128)(2,1)S(1)}) fusion(bf16[4,640,64]{2,1,0:T(8,128)(2,1)} %shard_map.113), kind=kLoop, calls=%fused_computation.119 | loop fusion | bytes 655360 | tf_op jit(solution)/shard_map/slice | solution.py:215
  70.6 0.7 dynamic_update_slice.13
  72.5 1.0 collective-permute-start.7
  73.4 3.5 %collective-permute-start.9 = (bf16[256,320]{0,1:T(8,128)(2,1)S(1)}, bf16[256,320]{0,1:T(8,128)(2,1)S(1)}, u32[]{:S(2)}, u32[]{:S(2)}) collective-permute-start(bf16[256,320]{0,1:T(8,128)(2,1)S(1)} %dynamic_update_slice.15), channel_id=1, source_target_pairs={{0,2},{1,3},{2,0},{3,1},{4,6},{5,7},{6,4},{7,5},{8,10},{9,11},{10,... | collective-permute-start | bytes 491528 | tf_op jit(solution)/shard_map/ppermute | solution.py:124
  76.9 1.3 %fusion.20 = f32[256,512]{1,0:T(8,128)S(1)} fusion(bf16[256,320]{0,1:T(8,128)(2,1)S(1)} %dynamic_update_slice.15, bf16[320,2048]{1,0:T(8,128)(2,1)} %param.14, s32[]{:T(128)S(6)} %select_n.125), kind=kOutput, calls=%fused_computation.37 | convolution fusion | flops 83886080 | bytes 1015812 | tf_op jit(solution)/shard_map/dot_general | solution.py:226
  78.2 7.0 %collective-permute-done.9 = bf16[256,320]{0,1:T(8,128)(2,1)S(1)} collective-permute-done((bf16[256,320]{0,1:T(8,128)(2,1)S(1)}, bf16[256,320]{0,1:T(8,128)(2,1)S(1)}, u32[]{:S(2)}, u32[]{:S(2)}) %collective-permute-start.9) | collective-permute-done | bytes 163872 | tf_op jit(solution)/shard_map/ppermute | solution.py:124
  85.5 1.3 %convolution_add_fusion.2 = f32[256,512]{1,0:T(8,128)S(1)} fusion(f32[256,512]{1,0:T(8,128)S(1)} %fusion.20, bf16[256,320]{0,1:T(8,128)(2,1)S(1)} %collective-permute-done.7, bf16[320,512]{1,0:T(8,128)(2,1)} %collective-permute-done.8), kind=kOutput, calls=%fused_computation.4 | convolution fusion | flops 84017152 | bytes 1540096 | tf_op jit(solution)/shard_map/dot_general | solution.py:226
  87.1 3.3 %collective-permute-done.11 = bf16[256,320]{0,1:T(8,128)(2,1)S(1)} collective-permute-done((bf16[256,320]{0,1:T(8,128)(2,1)S(1)}, bf16[256,320]{0,1:T(8,128)(2,1)S(1)}, u32[]{:S(2)}, u32[]{:S(2)}) %collective-permute-start.11) | collective-permute-done | bytes 163872 | tf_op jit(solution)/shard_map/ppermute | solution.py:124
  90.5 1.4 %fusion.3 = (f32[256]{0:T(256)S(1)}, bf16[256,512]{1,0:T(8,128)(2,1)S(1)}) fusion(f32[256,512]{1,0:T(8,128)S(1)} %convolution_add_fusion.1, bf16[256,320]{0,1:T(8,128)(2,1)S(1)} %collective-permute-done.11, bf16[320,512]{1,0:T(8,128)(2,1)} %collective-permute-done.12, bf16[256,512]{1,0:T(8,128)(2,1)S(1)} %copy-done.4), kind=kOutput, calls=%fused_computation.19 | convolution fusion | flops 84803328 | bytes 1541120 | tf_op jit(solution)/shard_map/dot_general | solution.py:226
  91.9 2.0 %collective-permute-start.14 = (bf16[256,512]{1,0:T(8,128)(2,1)S(1)}, bf16[256,512]{1,0:T(8,128)(2,1)S(1)}, u32[]{:S(2)}, u32[]{:S(2)}) collective-permute-start(bf16[256,512]{1,0:T(8,128)(2,1)S(1)} %get-tuple-element.52), channel_id=1, source_target_pairs={{0,2},{1,3},{2,0},{3,1},{4,6},{5,7},{6,4},{7,5},{8,10},{9,11},{10,... | collective-permute-start | bytes 786440 | tf_op jit(solution)/shard_map/ppermute | solution.py:124
  93.8 1.7 %collective-permute-start.13 = (bf16[256,512]{1,0:T(8,128)(2,1)S(1)}, bf16[256,512]{1,0:T(8,128)(2,1)S(1)}, u32[]{:S(2)}, u32[]{:S(2)}) collective-permute-start(bf16[256,512]{1,0:T(8,128)(2,1)S(1)} %get-tuple-element.52), channel_id=1, source_target_pairs={{0,1},{1,0},{2,3},{3,2},{4,5},{5,4},{6,7},{7,6},{8,9},{9,8},{10,11... | collective-permute-start | bytes 786440 | tf_op jit(solution)/shard_map/ppermute | solution.py:124
  95.6 9.7 %collective-permute-done.14 = bf16[256,512]{1,0:T(8,128)(2,1)S(1)} collective-permute-done((bf16[256,512]{1,0:T(8,128)(2,1)S(1)}, bf16[256,512]{1,0:T(8,128)(2,1)S(1)}, u32[]{:S(2)}, u32[]{:S(2)}) %collective-permute-start.14) | collective-permute-done | bytes 262176 | tf_op jit(solution)/shard_map/ppermute | solution.py:124
  105.3 0.6 collective-permute-start.15
  106.3 6.1 %collective-permute-done.15 = bf16[256,512]{1,0:T(8,128)(2,1)S(1)} collective-permute-done((bf16[256,512]{1,0:T(8,128)(2,1)S(1)}, bf16[256,512]{1,0:T(8,128)(2,1)S(1)}, u32[]{:S(2)}, u32[]{:S(2)}) %collective-permute-start.15) | collective-permute-done | bytes 262176 | tf_op jit(solution)/shard_map/ppermute | solution.py:124
  113.6 1.0 fusion.2
  (90 shorter events, 8.0 us)
Async XLA Ops:
  0.6 111.9 %copy-start = (bf16[2048,320]{0,1:T(8,128)(2,1)S(1)}, bf16[2048,320]{0,1:T(8,128)(2,1)}, u32[]{:S(2)}) copy-start(bf16[2048,320]{0,1:T(8,128)(2,1)} %param.16) | copy-start | bytes 3932164
  0.6 10.4 %copy-start.10 = (s32[1,4]{1,0:T(1,128)S(1)}, s32[1,4]{1,0:T(1,128)}, u32[]{:S(2)}) copy-start(s32[1,4]{1,0:T(1,128)} %param.17) | copy-start | bytes 52
  0.7 17.6 %copy-start.11 = (s32[1,4]{1,0:T(1,128)S(1)}, s32[1,4]{1,0:T(1,128)}, u32[]{:S(2)}) copy-start(s32[1,4]{1,0:T(1,128)} %param.18) | copy-start | bytes 52
  0.7 20.1 %copy-start.2 = (bf16[256,320]{0,1:T(8,128)(2,1)S(1)}, bf16[256,320]{0,1:T(8,128)(2,1)}, u32[]{:S(2)}) copy-start(bf16[256,320]{0,1:T(8,128)(2,1)} %param.11) | copy-start | bytes 491524
  2.3 43.4 %collective-permute-start = (bf16[1024,256]{1,0:T(8,128)(2,1)S(1)}, bf16[1024,256]{1,0:T(8,128)(2,1)}, u32[]{:S(2)}, u32[]{:S(2)}) collective-permute-start(bf16[1024,256]{1,0:T(8,128)(2,1)S(1)} %copy.28), channel_id=1, source_target_pairs={{0,4},{4,0},{8,12},{12,8},{16,20},{20,16},{24,28},{28,24},{1,5},{5... | collective-permute-start | bytes 1572872 | tf_op jit(solution)/shard_map/ppermute | solution.py:34
  2.8 35.7 %collective-permute-start.1 = (bf16[1024,256]{1,0:T(8,128)(2,1)S(1)}, bf16[1024,256]{1,0:T(8,128)(2,1)}, u32[]{:S(2)}, u32[]{:S(2)}) collective-permute-start(bf16[1024,256]{1,0:T(8,128)(2,1)S(1)} %copy.28), channel_id=1, source_target_pairs={{0,8},{4,12},{8,0},{12,4},{16,24},{20,28},{24,16},{28,20},{1,9},{5... | collective-permute-start | bytes 1572872 | tf_op jit(solution)/shard_map/ppermute | solution.py:34
  5.4 36.0 %collective-permute-start.3 = (bf16[1024,256]{1,0:T(8,128)(2,1)S(1)}, bf16[1024,256]{1,0:T(8,128)(2,1)}, u32[]{:S(2)}, u32[]{:S(2)}) collective-permute-start(bf16[1024,256]{1,0:T(8,128)(2,1)S(1)} %copy.28), channel_id=1, source_target_pairs={{0,16},{4,20},{8,24},{12,28},{16,0},{20,4},{24,8},{28,12},{1,17},{... | collective-permute-start | bytes 1572872 | tf_op jit(solution)/shard_map/ppermute | solution.py:34
  6.9 41.4 %collective-permute-start.5 = (bf16[1024,256]{1,0:T(8,128)(2,1)S(1)}, bf16[1024,256]{1,0:T(8,128)(2,1)}, u32[]{:S(2)}, u32[]{:S(2)}) collective-permute-start(bf16[1024,256]{1,0:T(8,128)(2,1)S(1)} %copy.28), channel_id=1, source_target_pairs={{0,24},{4,28},{8,16},{12,20},{16,8},{20,12},{24,0},{28,4},{1,25},{... | collective-permute-start | bytes 1572872 | tf_op jit(solution)/shard_map/ppermute | solution.py:34
  9.1 76.4 %collective-permute-start.8 = (bf16[320,512]{1,0:T(8,128)(2,1)}, bf16[320,512]{1,0:T(8,128)(2,1)}, u32[]{:S(2)}, u32[]{:S(2)}) collective-permute-start(bf16[320,512]{1,0:T(8,128)(2,1)} %get-tuple-element.5), channel_id=1, source_target_pairs={{0,1},{1,0},{2,3},{3,2},{4,5},{5,4},{6,7},{7,6},{8,9},{9,8},{10,11... | collective-permute-start | bytes 983048 | tf_op jit(solution)/shard_map/ppermute | solution.py:124
  11.3 27.2 %copy-start.5 = (s32[4]{0:T(128)}, s32[4]{0:T(128)S(1)}, u32[]{:S(2)}) copy-start(s32[4]{0:T(128)S(1)} %get-tuple-element.2.first_ref) | copy-start | bytes 52
  11.3 27.2 %copy-start.6 = (s32[4]{0:T(128)}, s32[4]{0:T(128)S(1)}, u32[]{:S(2)}) copy-start(s32[4]{0:T(128)S(1)} %get-tuple-element.3.start_ref) | copy-start | bytes 52
  24.4 27.7 %copy-start.3 = (bf16[320,512]{1,0:T(8,128)(2,1)S(1)}, bf16[320,512]{1,0:T(8,128)(2,1)}, u32[]{:S(2)}) copy-start(bf16[320,512]{1,0:T(8,128)(2,1)} %get-tuple-element.4) | copy-start | bytes 983044
  38.5 13.6 %collective-permute-start.2 = (bf16[1024,256]{1,0:T(8,128)(2,1)}, bf16[1024,256]{1,0:T(8,128)(2,1)S(1)}, u32[]{:S(2)}, u32[]{:S(2)}) collective-permute-start(bf16[1024,256]{1,0:T(8,128)(2,1)} %collective-permute-done.1), channel_id=1, source_target_pairs={{0,4},{4,0},{8,12},{12,8},{16,20},{20,16},{24,28},{28,24},{1,5},{5... | collective-permute-start | bytes 1572872 | tf_op jit(solution)/shard_map/ppermute | solution.py:34
  41.4 13.4 %collective-permute-start.4 = (bf16[1024,256]{1,0:T(8,128)(2,1)}, bf16[1024,256]{1,0:T(8,128)(2,1)S(1)}, u32[]{:S(2)}, u32[]{:S(2)}) collective-permute-start(bf16[1024,256]{1,0:T(8,128)(2,1)} %collective-permute-done.3), channel_id=1, source_target_pairs={{0,4},{4,0},{8,12},{12,8},{16,20},{20,16},{24,28},{28,24},{1,5},{5... | collective-permute-start | bytes 1572872 | tf_op jit(solution)/shard_map/ppermute | solution.py:34
  45.7 41.1 %collective-permute-start.10 = (bf16[320,512]{1,0:T(8,128)(2,1)}, bf16[320,512]{1,0:T(8,128)(2,1)S(1)}, u32[]{:S(2)}, u32[]{:S(2)}) collective-permute-start(bf16[320,512]{1,0:T(8,128)(2,1)} %get-tuple-element.6), channel_id=1, source_target_pairs={{0,2},{1,3},{2,0},{3,1},{4,6},{5,7},{6,4},{7,5},{8,10},{9,11},{10,... | collective-permute-start | bytes 983048 | tf_op jit(solution)/shard_map/ppermute | solution.py:124
  48.3 9.2 %collective-permute-start.6 = (bf16[1024,256]{1,0:T(8,128)(2,1)}, bf16[1024,256]{1,0:T(8,128)(2,1)S(1)}, u32[]{:S(2)}, u32[]{:S(2)}) collective-permute-start(bf16[1024,256]{1,0:T(8,128)(2,1)} %collective-permute-done.5), channel_id=1, source_target_pairs={{0,4},{4,0},{8,12},{12,8},{16,20},{20,16},{24,28},{28,24},{1,5},{5... | collective-permute-start | bytes 1572872 | tf_op jit(solution)/shard_map/ppermute | solution.py:34
  52.1 35.1 %collective-permute-start.12 = (bf16[320,512]{1,0:T(8,128)(2,1)S(1)}, bf16[320,512]{1,0:T(8,128)(2,1)}, u32[]{:S(2)}, u32[]{:S(2)}) collective-permute-start(bf16[320,512]{1,0:T(8,128)(2,1)S(1)} %copy-done.3), channel_id=1, source_target_pairs={{0,3},{1,2},{2,1},{3,0},{4,7},{5,6},{6,5},{7,4},{8,11},{9,10},{10,... | collective-permute-start | bytes 983048 | tf_op jit(solution)/shard_map/ppermute | solution.py:124
  58.3 11.7 %copy-start.9 = (pred[128]{0:T(512)(128)(4,1)S(1)}, pred[128]{0:T(512)(128)(4,1)}, u32[]{:S(2)}) copy-start(pred[128]{0:T(512)(128)(4,1)} %compare_and_fusion.3) | copy-start | bytes 388
  58.3 12.2 %copy-start.8 = (pred[128]{0:T(512)(128)(4,1)S(1)}, pred[128]{0:T(512)(128)(4,1)}, u32[]{:S(2)}) copy-start(pred[128]{0:T(512)(128)(4,1)} %compare_and_fusion.2) | copy-start | bytes 388
  68.5 21.9 %copy-start.4 = (bf16[256,512]{1,0:T(8,128)(2,1)S(1)}, bf16[256,512]{1,0:T(8,128)(2,1)}, u32[]{:S(2)}) copy-start(bf16[256,512]{1,0:T(8,128)(2,1)} %param.10) | copy-start | bytes 786436
  69.8 36.1 %copy-start.7 = (bf16[2048]{0:T(1024)(128)(2,1)S(1)}, bf16[2048]{0:T(1024)(128)(2,1)}, u32[]{:S(2)}) copy-start(bf16[2048]{0:T(1024)(128)(2,1)} %param.15) | copy-start | bytes 12292
  72.5 13.0 %collective-permute-start.7 = (bf16[256,320]{0,1:T(8,128)(2,1)S(1)}, bf16[256,320]{0,1:T(8,128)(2,1)S(1)}, u32[]{:S(2)}, u32[]{:S(2)}) collective-permute-start(bf16[256,320]{0,1:T(8,128)(2,1)S(1)} %dynamic_update_slice.15), channel_id=1, source_target_pairs={{0,1},{1,0},{2,3},{3,2},{4,5},{5,4},{6,7},{7,6},{8,9},{9,8},{10,11... | collective-permute-start | bytes 491528 | tf_op jit(solution)/shard_map/ppermute | solution.py:124
  73.4 11.7 %collective-permute-start.9 = (bf16[256,320]{0,1:T(8,128)(2,1)S(1)}, bf16[256,320]{0,1:T(8,128)(2,1)S(1)}, u32[]{:S(2)}, u32[]{:S(2)}) collective-permute-start(bf16[256,320]{0,1:T(8,128)(2,1)S(1)} %dynamic_update_slice.15), channel_id=1, source_target_pairs={{0,2},{1,3},{2,0},{3,1},{4,6},{5,7},{6,4},{7,5},{8,10},{9,11},{10,... | collective-permute-start | bytes 491528 | tf_op jit(solution)/shard_map/ppermute | solution.py:124
  85.1 5.3 %collective-permute-start.11 = (bf16[256,320]{0,1:T(8,128)(2,1)S(1)}, bf16[256,320]{0,1:T(8,128)(2,1)S(1)}, u32[]{:S(2)}, u32[]{:S(2)}) collective-permute-start(bf16[256,320]{0,1:T(8,128)(2,1)S(1)} %collective-permute-done.9), channel_id=1, source_target_pairs={{0,1},{1,0},{2,3},{3,2},{4,5},{5,4},{6,7},{7,6},{8,9},{9,8},{10,11... | collective-permute-start | bytes 491528 | tf_op jit(solution)/shard_map/ppermute | solution.py:124
  91.9 22.8 %copy-start.1 = (bf16[256,512]{1,0:T(8,128)(2,1)}, bf16[256,512]{1,0:T(8,128)(2,1)S(1)}, u32[]{:S(2)}) copy-start(bf16[256,512]{1,0:T(8,128)(2,1)S(1)} %get-tuple-element.52) | copy-start | bytes 786436
  91.9 13.4 %collective-permute-start.14 = (bf16[256,512]{1,0:T(8,128)(2,1)S(1)}, bf16[256,512]{1,0:T(8,128)(2,1)S(1)}, u32[]{:S(2)}, u32[]{:S(2)}) collective-permute-start(bf16[256,512]{1,0:T(8,128)(2,1)S(1)} %get-tuple-element.52), channel_id=1, source_target_pairs={{0,2},{1,3},{2,0},{3,1},{4,6},{5,7},{6,4},{7,5},{8,10},{9,11},{10,... | collective-permute-start | bytes 786440 | tf_op jit(solution)/shard_map/ppermute | solution.py:124
  93.8 12.3 %collective-permute-start.13 = (bf16[256,512]{1,0:T(8,128)(2,1)S(1)}, bf16[256,512]{1,0:T(8,128)(2,1)S(1)}, u32[]{:S(2)}, u32[]{:S(2)}) collective-permute-start(bf16[256,512]{1,0:T(8,128)(2,1)S(1)} %get-tuple-element.52), channel_id=1, source_target_pairs={{0,1},{1,0},{2,3},{3,2},{4,5},{5,4},{6,7},{7,6},{8,9},{9,8},{10,11... | collective-permute-start | bytes 786440 | tf_op jit(solution)/shard_map/ppermute | solution.py:124
  105.3 7.0 %collective-permute-start.15 = (bf16[256,512]{1,0:T(8,128)(2,1)S(1)}, bf16[256,512]{1,0:T(8,128)(2,1)S(1)}, u32[]{:S(2)}, u32[]{:S(2)}) collective-permute-start(bf16[256,512]{1,0:T(8,128)(2,1)S(1)} %collective-permute-done.14), channel_id=1, source_target_pairs={{0,1},{1,0},{2,3},{3,2},{4,5},{5,4},{6,7},{7,6},{8,9},{9,8},{10,11... | collective-permute-start | bytes 786440 | tf_op jit(solution)/shard_map/ppermute | solution.py:124

commit v2 on v0

--- a/solution.py
+++ b/solution.py
@@ -88,10 +88,8 @@
     ) + jnp.dot(
         suffix_weights.astype(jnp.bfloat16), suffix_values, preferred_element_type=jnp.float32
     )
-    attended = accumulated / denominator
-    first_pair = attended[:, :HD]
-    second_pair = attended[:, HD:]
-    out_ref[...] = jnp.where(pair_ref[...] > 0, second_pair, first_pair).astype(out_ref.dtype)
+    picked = jnp.where(pair_ref[...] > 0, accumulated[:, HD:], accumulated[:, :HD])
+    out_ref[...] = (picked / denominator).astype(out_ref.dtype)
 
 
 def window_attention(

time: 104 us -> 104 us (level)
  the two profiles are of different devices: /device:TPU:8 before, /device:TPU:0 now
where the time goes in v2:
time: 104 us; the launch traced here: 103 us
  local copies, waits for them, and re-layouts  26.1 us (25%)
  waiting for transfers between devices  26 us (25%)
  starting transfers between devices  20.1 us (19%)
  Pallas kernels  10.1 us (10%)
  between operations  8.71 us (8%)
  matrix products  7.37 us (7%)
  other arithmetic  5.14 us (5%)
    ppermute x9, waiting for transfers between devices, xor_tp(): return lax.ppermute(block, 'tp', pairs)  25.1 us
    ppermute x9, starting transfers between devices, xor_tp(): return lax.ppermute(block, 'tp', pairs)  15.2 us
    unnamed x32, local copies, waits for them, and re-layouts  13.4 us
    pallas_call x1, Pallas kernels, window_attention(): pl.pallas_call(attention_kernel, grid_spec=grid_spec, out_shape=jax.Shape...  10.1 us
    dot_general x4, matrix products, local(): jnp.dot(head_blocks[mask], weight_pieces[mask], preferred_element_type=jn...  5.27 us
    ppermute x7, starting transfers between devices, xor_permute(): return lax.ppermute(block, 'req', pairs)  4.84 us
    dynamic_slice x1, local copies, waits for them, and re-layouts, local(): piece = lax.dynamic_slice_in_dim(out_weight, partner * width, width, 1)  2.16 us
    dot_general x4, matrix products, local(): part = jnp.dot(normed, block_weight, preferred_element_type=jnp.float32)  2.1 us
  transfers between devices with their start and end apart: 16, of which 5 were waited for; matrix products, arithmetic and copies ran while one was open for 32% of the time, Pallas kernels for 10%

profile of v2, /device:TPU:0, one launch (start us, length us, event | category | flops | bytes accessed | tf_op | source)
XLA Modules:
  0.0 103.5 jit_solution(3661681208402871794)
XLA Ops:
  0.7 1.4 %copy.48 = bf16[1024,1,256]{0,2,1:T(8,128)(2,1)S(1)} copy(bf16[1024,1,256]{2,0,1:T(8,128)(2,1)} %param.13) | data formatting | bytes 1048576 | tf_op args[3]
  2.3 0.5 collective-permute-start
  2.8 2.6 %collective-permute-start.1 = (bf16[1024,256]{1,0:T(8,128)(2,1)S(1)}, bf16[1024,256]{1,0:T(8,128)(2,1)}, u32[]{:S(2)}, u32[]{:S(2)}) collective-permute-start(bf16[1024,256]{1,0:T(8,128)(2,1)S(1)} %copy.54), channel_id=1, source_target_pairs={{0,8},{4,12},{8,0},{12,4},{16,24},{20,28},{24,16},{28,20},{1,9},{5... | collective-permute-start | bytes 1572872 | tf_op jit(solution)/shard_map/ppermute | solution.py:34
  5.4 1.5 %collective-permute-start.3 = (bf16[1024,256]{1,0:T(8,128)(2,1)S(1)}, bf16[1024,256]{1,0:T(8,128)(2,1)}, u32[]{:S(2)}, u32[]{:S(2)}) collective-permute-start(bf16[1024,256]{1,0:T(8,128)(2,1)S(1)} %copy.54), channel_id=1, source_target_pairs={{0,16},{4,20},{8,24},{12,28},{16,0},{20,4},{24,8},{28,12},{1,17},{... | collective-permute-start | bytes 1572872 | tf_op jit(solution)/shard_map/ppermute | solution.py:34
  6.9 2.2 %constant_dynamic-slice_fusion = (bf16[320,512]{1,0:T(8,128)(2,1)}, bf16[320,512]{1,0:T(8,128)(2,1)}, bf16[320,512]{1,0:T(8,128)(2,1)}) fusion(bf16[320,2048]{1,0:T(8,128)(2,1)} %param.14, s32[]{:T(128)S(6)} %select_n.131, s32[]{:T(128)S(6)} %select_n.129, s32[]{:T(128)S(6)} %select_n.130), kind=kLoop, calls=%fused_computation.80 | loop fusion | bytes 1966092 | tf_op jit(solution)/shard_map/dynamic_slice | solution.py:160
  9.1 2.0 %collective-permute-start.8 = (bf16[320,512]{1,0:T(8,128)(2,1)}, bf16[320,512]{1,0:T(8,128)(2,1)}, u32[]{:S(2)}, u32[]{:S(2)}) collective-permute-start(bf16[320,512]{1,0:T(8,128)(2,1)} %get-tuple-element.5), channel_id=1, source_target_pairs={{0,1},{1,0},{2,3},{3,2},{4,5},{5,4},{6,7},{7,6},{8,9},{9,8},{10,11... | collective-permute-start | bytes 983048 | tf_op jit(solution)/shard_map/ppermute | solution.py:122
  11.3 0.5 broadcast_minimum_fusion
  11.8 0.6 fusion.47
  20.7 0.8 add_select_fusion.row_ref
  23.4 1.0 %copy.55 = bf16[256,1,256]{0,2,1:T(8,128)(2,1)S(1)} copy(bf16[256,1,256]{2,0,1:T(8,128)(2,1)} %param.12) | data formatting | bytes 262144 | tf_op args[2]
  24.9 0.7 copy.58
  25.6 0.7 copy.57
  26.4 0.8 constant_dynamic-update-slice_fusion.7
  27.2 1.6 %pad_maximum_fusion.1.suffix_ref = bf16[4,128,256]{2,1,0:T(8,128)(2,1)} fusion(bf16[1,128,256]{2,1,0:T(8,128)(2,1)S(1)} %bitcast.114, bf16[1,128,256]{2,1,0:T(8,128)(2,1)S(1)} %bitcast.115, bf16[1,128,256]{2,1,0:T(8,128)(2,1)} %bitcast.116, bf16[1,128,256]{2,1,0:T(8,128)(2,1)} %bitcast.117), kind=kLoop, calls=%fused_computation.43 | loop fusion | flops 393216 | bytes 524288 | tf_op jit(solution)/shard_map/stack | solution.py:205
  28.8 0.9 pad_maximum_fusion.query_ref
  29.8 0.9 collective-permute-done.3
  30.7 0.9 copy.67
  31.8 1.1 %gather_fusion = s32[4]{0:T(128)} fusion(s32[4]{0:T(128)S(1)} %fusion.42, s32[1024]{0:T(1024)S(1)} %pad_clamp_fusion), kind=kCustom, calls=%fused_computation | custom fusion | bytes 48 | tf_op jit(solution)/shard_map/gather | solution.py:198
  32.9 2.6 %collective-permute-start.10 = (bf16[320,512]{1,0:T(8,128)(2,1)}, bf16[320,512]{1,0:T(8,128)(2,1)}, u32[]{:S(2)}, u32[]{:S(2)}) collective-permute-start(bf16[320,512]{1,0:T(8,128)(2,1)} %get-tuple-element.6), channel_id=1, source_target_pairs={{0,2},{1,3},{2,0},{3,1},{4,6},{5,7},{6,4},{7,5},{8,10},{9,11},{10,... | collective-permute-start | bytes 983048 | tf_op jit(solution)/shard_map/ppermute | solution.py:122
  35.7 1.9 %constant_dynamic-update-slice_fusion.6 = bf16[8192,256]{1,0:T(8,128)(2,1)} fusion(bf16[8192,256]{1,0:T(8,128)(2,1)} %constant_dynamic-update-slice_fusion.7, bf16[1024,256]{1,0:T(8,128)(2,1)} %collective-permute-done), kind=kLoop, calls=%fused_computation.72 | loop fusion | bytes 1048576
  37.6 1.9 %constant_dynamic-update-slice_fusion.5 = bf16[8192,256]{1,0:T(8,128)(2,1)} fusion(bf16[8192,256]{1,0:T(8,128)(2,1)} %constant_dynamic-update-slice_fusion.6, bf16[1024,256]{1,0:T(8,128)(2,1)} %collective-permute-done.1), kind=kLoop, calls=%fused_computation.71 | loop fusion | bytes 1048576
  39.5 1.4 %collective-permute-start.12 = (bf16[320,512]{1,0:T(8,128)(2,1)S(1)}, bf16[320,512]{1,0:T(8,128)(2,1)}, u32[]{:S(2)}, u32[]{:S(2)}) collective-permute-start(bf16[320,512]{1,0:T(8,128)(2,1)S(1)} %copy-done.3), channel_id=1, source_target_pairs={{0,3},{1,2},{2,1},{3,0},{4,7},{5,6},{6,5},{7,4},{8,11},{9,10},{10,... | collective-permute-start | bytes 983048 | tf_op jit(solution)/shard_map/ppermute | solution.py:122
  40.8 0.9 constant_dynamic-update-slice_fusion.4
  41.7 1.9 %constant_dynamic-update-slice_fusion.3 = bf16[8192,256]{1,0:T(8,128)(2,1)} fusion(bf16[8192,256]{1,0:T(8,128)(2,1)} %constant_dynamic-update-slice_fusion.4, bf16[1024,256]{1,0:T(8,128)(2,1)} %collective-permute-done.3), kind=kLoop, calls=%fused_computation.69 | loop fusion | bytes 1048576
  43.5 0.8 constant_dynamic-update-slice_fusion.2
  44.4 1.9 %constant_dynamic-update-slice_fusion.1 = bf16[8192,256]{1,0:T(8,128)(2,1)} fusion(bf16[8192,256]{1,0:T(8,128)(2,1)} %constant_dynamic-update-slice_fusion.2, bf16[1024,256]{1,0:T(8,128)(2,1)} %collective-permute-done.5), kind=kLoop, calls=%fused_computation.67 | loop fusion | bytes 1048576
  46.2 0.8 constant_dynamic-update-slice_fusion.prefix_ref
  47.1 10.1 %shard_map.113 = bf16[4,640,64]{2,1,0:T(8,128)(2,1)} custom-call(s32[4]{0:T(128)} %gather_fusion, s32[4]{0:T(128)} %copy-done.5, s32[4]{0:T(128)} %get-tuple-element.3.start_ref, bf16[4,640,128]{2,1,0:T(8,128)(2,1)} %pad_maximum_fusion.query_ref, bf16[8192,256]{1,0:T(8,128)(2,1)} %constant_dynamic-update-slice_fusion.prefix_ref, ...), custom_call_target="tpu_custom_call" | custom-call | tf_op jit(solution)/shard_map/pallas_call | solution.py:113
  57.2 1.2 %fusion.45 = (bf16[1,640,64]{2,1,0:T(8,128)(2,1)S(1)}, bf16[1,640,64]{2,1,0:T(8,128)(2,1)S(1)}, bf16[1,640,64]{2,1,0:T(8,128)(2,1)S(1)}, bf16[1,640,64]{2,1,0:T(8,128)(2,1)S(1)}) fusion(bf16[4,640,64]{2,1,0:T(8,128)(2,1)} %shard_map.113), kind=kLoop, calls=%fused_computation.119 | loop fusion | bytes 655360 | tf_op jit(solution)/shard_map/slice | solution.py:212
  59.3 0.7 dynamic_update_slice.11
  60.0 0.7 dynamic_update_slice.12
  60.8 0.4 select_n.124
  61.5 2.8 %collective-permute-start.9 = (bf16[256,320]{0,1:T(8,128)(2,1)S(1)}, bf16[256,320]{0,1:T(8,128)(2,1)S(1)}, u32[]{:S(2)}, u32[]{:S(2)}) collective-permute-start(bf16[256,320]{0,1:T(8,128)(2,1)S(1)} %select_select_fusion), channel_id=1, source_target_pairs={{0,2},{1,3},{2,0},{3,1},{4,6},{5,7},{6,4},{7,5},{8,10},{9,11},{10,... | collective-permute-start | bytes 491528 | tf_op jit(solution)/shard_map/ppermute | solution.py:122
  64.3 1.3 %fusion.20 = f32[256,512]{1,0:T(8,128)S(1)} fusion(bf16[256,320]{0,1:T(8,128)(2,1)S(1)} %select_select_fusion, bf16[320,2048]{1,0:T(8,128)(2,1)} %param.14, s32[]{:T(128)S(6)} %select_n.128), kind=kOutput, calls=%fused_computation.37 | convolution fusion | flops 83886080 | bytes 1015812 | tf_op jit(solution)/shard_map/dot_general | solution.py:221
  65.6 6.7 %collective-permute-done.9 = bf16[256,320]{0,1:T(8,128)(2,1)S(1)} collective-permute-done((bf16[256,320]{0,1:T(8,128)(2,1)S(1)}, bf16[256,320]{0,1:T(8,128)(2,1)S(1)}, u32[]{:S(2)}, u32[]{:S(2)}) %collective-permute-start.9) | collective-permute-done | bytes 163872 | tf_op jit(solution)/shard_map/ppermute | solution.py:122
  72.3 0.6 collective-permute-start.11
  72.9 1.3 %convolution_add_fusion.2 = f32[256,512]{1,0:T(8,128)S(1)} fusion(f32[256,512]{1,0:T(8,128)S(1)} %fusion.20, bf16[256,320]{0,1:T(8,128)(2,1)S(1)} %collective-permute-done.7, bf16[320,512]{1,0:T(8,128)(2,1)} %collective-permute-done.8), kind=kOutput, calls=%fused_computation.4 | convolution fusion | flops 84017152 | bytes 1540096 | tf_op jit(solution)/shard_map/dot_general | solution.py:221
  74.2 1.3 %convolution_add_fusion.1 = f32[256,512]{1,0:T(8,128)S(1)} fusion(f32[256,512]{1,0:T(8,128)S(1)} %convolution_add_fusion.2, bf16[256,320]{0,1:T(8,128)(2,1)S(1)} %collective-permute-done.9, bf16[320,512]{1,0:T(8,128)(2,1)} %collective-permute-done.10), kind=kOutput, calls=%fused_computation.3 | convolution fusion | flops 84017152 | bytes 1540096 | tf_op jit(solution)/shard_map/dot_general | solution.py:221
  75.5 2.0 %collective-permute-done.11 = bf16[256,320]{0,1:T(8,128)(2,1)S(1)} collective-permute-done((bf16[256,320]{0,1:T(8,128)(2,1)S(1)}, bf16[256,320]{0,1:T(8,128)(2,1)S(1)}, u32[]{:S(2)}, u32[]{:S(2)}) %collective-permute-start.11) | collective-permute-done | bytes 163872 | tf_op jit(solution)/shard_map/ppermute | solution.py:122
  77.6 1.4 %fusion.3 = (f32[256]{0:T(256)S(1)}, bf16[256,512]{1,0:T(8,128)(2,1)S(1)}) fusion(f32[256,512]{1,0:T(8,128)S(1)} %convolution_add_fusion.1, bf16[256,320]{0,1:T(8,128)(2,1)S(1)} %collective-permute-done.11, bf16[320,512]{1,0:T(8,128)(2,1)} %collective-permute-done.12, bf16[256,512]{1,0:T(8,128)(2,1)S(1)} %copy-done.4), kind=kOutput, calls=%fused_computation.19 | convolution fusion | flops 84803328 | bytes 1541120 | tf_op jit(solution)/shard_map/dot_general | solution.py:221
  79.0 3.2 %collective-permute-start.14 = (bf16[256,512]{1,0:T(8,128)(2,1)S(1)}, bf16[256,512]{1,0:T(8,128)(2,1)S(1)}, u32[]{:S(2)}, u32[]{:S(2)}) collective-permute-start(bf16[256,512]{1,0:T(8,128)(2,1)S(1)} %get-tuple-element.48), channel_id=1, source_target_pairs={{0,2},{1,3},{2,0},{3,1},{4,6},{5,7},{6,4},{7,5},{8,10},{9,11},{10,... | collective-permute-start | bytes 786440 | tf_op jit(solution)/shard_map/ppermute | solution.py:122
  82.2 1.7 %collective-permute-start.13 = (bf16[256,512]{1,0:T(8,128)(2,1)S(1)}, bf16[256,512]{1,0:T(8,128)(2,1)S(1)}, u32[]{:S(2)}, u32[]{:S(2)}) collective-permute-start(bf16[256,512]{1,0:T(8,128)(2,1)S(1)} %get-tuple-element.48), channel_id=1, source_target_pairs={{0,1},{1,0},{2,3},{3,2},{4,5},{5,4},{6,7},{7,6},{8,9},{9,8},{10,11... | collective-permute-start | bytes 786440 | tf_op jit(solution)/shard_map/ppermute | solution.py:122
  83.9 10.0 %collective-permute-done.14 = bf16[256,512]{1,0:T(8,128)(2,1)S(1)} collective-permute-done((bf16[256,512]{1,0:T(8,128)(2,1)S(1)}, bf16[256,512]{1,0:T(8,128)(2,1)S(1)}, u32[]{:S(2)}, u32[]{:S(2)}) %collective-permute-start.14) | collective-permute-done | bytes 262176 | tf_op jit(solution)/shard_map/ppermute | solution.py:122
  93.9 0.6 collective-permute-start.15
  94.9 6.4 %collective-permute-done.15 = bf16[256,512]{1,0:T(8,128)(2,1)S(1)} collective-permute-done((bf16[256,512]{1,0:T(8,128)(2,1)S(1)}, bf16[256,512]{1,0:T(8,128)(2,1)S(1)}, u32[]{:S(2)}, u32[]{:S(2)}) %collective-permute-start.15) | collective-permute-done | bytes 262176 | tf_op jit(solution)/shard_map/ppermute | solution.py:122
  101.4 0.4 fusion.18
  102.1 0.4 convolution_add_fusion.4
  102.5 1.0 fusion.2
  (83 shorter events, 5.7 us)
Async XLA Ops:
  0.6 100.7 %copy-start = (bf16[2048,320]{0,1:T(8,128)(2,1)S(1)}, bf16[2048,320]{0,1:T(8,128)(2,1)}, u32[]{:S(2)}) copy-start(bf16[2048,320]{0,1:T(8,128)(2,1)} %param.16) | copy-start | bytes 3932164
  0.6 10.5 %copy-start.7 = (s32[1,4]{1,0:T(1,128)S(1)}, s32[1,4]{1,0:T(1,128)}, u32[]{:S(2)}) copy-start(s32[1,4]{1,0:T(1,128)} %param.17) | copy-start | bytes 52
  0.7 17.0 %copy-start.9 = (s32[1,4]{1,0:T(1,128)S(1)}, s32[1,4]{1,0:T(1,128)}, u32[]{:S(2)}) copy-start(s32[1,4]{1,0:T(1,128)} %param.18) | copy-start | bytes 52
  0.7 19.7 %copy-start.8 = (s32[4]{0:T(128)S(1)}, s32[4]{0:T(128)}, u32[]{:S(2)}) copy-start(s32[4]{0:T(128)} %param.19) | copy-start | bytes 52
  0.7 19.7 %copy-start.2 = (bf16[256,320]{0,1:T(8,128)(2,1)S(1)}, bf16[256,320]{0,1:T(8,128)(2,1)}, u32[]{:S(2)}) copy-start(bf16[256,320]{0,1:T(8,128)(2,1)} %param.11) | copy-start | bytes 491524
  2.3 30.6 %collective-permute-start = (bf16[1024,256]{1,0:T(8,128)(2,1)S(1)}, bf16[1024,256]{1,0:T(8,128)(2,1)}, u32[]{:S(2)}, u32[]{:S(2)}) collective-permute-start(bf16[1024,256]{1,0:T(8,128)(2,1)S(1)} %copy.54), channel_id=1, source_target_pairs={{0,4},{4,0},{8,12},{12,8},{16,20},{20,16},{24,28},{28,24},{1,5},{5... | collective-permute-start | bytes 1572872 | tf_op jit(solution)/shard_map/ppermute | solution.py:34
  2.8 24.4 %collective-permute-start.1 = (bf16[1024,256]{1,0:T(8,128)(2,1)S(1)}, bf16[1024,256]{1,0:T(8,128)(2,1)}, u32[]{:S(2)}, u32[]{:S(2)}) collective-permute-start(bf16[1024,256]{1,0:T(8,128)(2,1)S(1)} %copy.54), channel_id=1, source_target_pairs={{0,8},{4,12},{8,0},{12,4},{16,24},{20,28},{24,16},{28,20},{1,9},{5... | collective-permute-start | bytes 1572872 | tf_op jit(solution)/shard_map/ppermute | solution.py:34
  5.4 25.3 %collective-permute-start.3 = (bf16[1024,256]{1,0:T(8,128)(2,1)S(1)}, bf16[1024,256]{1,0:T(8,128)(2,1)}, u32[]{:S(2)}, u32[]{:S(2)}) collective-permute-start(bf16[1024,256]{1,0:T(8,128)(2,1)S(1)} %copy.54), channel_id=1, source_target_pairs={{0,16},{4,20},{8,24},{12,28},{16,0},{20,4},{24,8},{28,12},{1,17},{... | collective-permute-start | bytes 1572872 | tf_op jit(solution)/shard_map/ppermute | solution.py:34
  6.9 28.6 %collective-permute-start.5 = (bf16[1024,256]{1,0:T(8,128)(2,1)S(1)}, bf16[1024,256]{1,0:T(8,128)(2,1)}, u32[]{:S(2)}, u32[]{:S(2)}) collective-permute-start(bf16[1024,256]{1,0:T(8,128)(2,1)S(1)} %copy.54), channel_id=1, source_target_pairs={{0,24},{4,28},{8,16},{12,20},{16,8},{20,12},{24,0},{28,4},{1,25},{... | collective-permute-start | bytes 1572872 | tf_op jit(solution)/shard_map/ppermute | solution.py:34
  9.1 63.8 %collective-permute-start.8 = (bf16[320,512]{1,0:T(8,128)(2,1)}, bf16[320,512]{1,0:T(8,128)(2,1)}, u32[]{:S(2)}, u32[]{:S(2)}) collective-permute-start(bf16[320,512]{1,0:T(8,128)(2,1)} %get-tuple-element.5), channel_id=1, source_target_pairs={{0,1},{1,0},{2,3},{3,2},{4,5},{5,4},{6,7},{7,6},{8,9},{9,8},{10,11... | collective-permute-start | bytes 983048 | tf_op jit(solution)/shard_map/ppermute | solution.py:122
  11.8 15.4 %copy-start.5 = (s32[4]{0:T(128)}, s32[4]{0:T(128)S(1)}, u32[]{:S(2)}) copy-start(s32[4]{0:T(128)S(1)} %get-tuple-element.2.first_ref) | copy-start | bytes 52
  23.4 16.0 %copy-start.3 = (bf16[320,512]{1,0:T(8,128)(2,1)S(1)}, bf16[320,512]{1,0:T(8,128)(2,1)}, u32[]{:S(2)}) copy-start(bf16[320,512]{1,0:T(8,128)(2,1)} %get-tuple-element.4) | copy-start | bytes 983044
  27.2 12.2 %collective-permute-start.2 = (bf16[1024,256]{1,0:T(8,128)(2,1)}, bf16[1024,256]{1,0:T(8,128)(2,1)S(1)}, u32[]{:S(2)}, u32[]{:S(2)}) collective-permute-start(bf16[1024,256]{1,0:T(8,128)(2,1)} %collective-permute-done.1), channel_id=1, source_target_pairs={{0,4},{4,0},{8,12},{12,8},{16,20},{20,16},{24,28},{28,24},{1,5},{5... | collective-permute-start | bytes 1572872 | tf_op jit(solution)/shard_map/ppermute | solution.py:34
  30.7 12.8 %collective-permute-start.4 = (bf16[1024,256]{1,0:T(8,128)(2,1)}, bf16[1024,256]{1,0:T(8,128)(2,1)S(1)}, u32[]{:S(2)}, u32[]{:S(2)}) collective-permute-start(bf16[1024,256]{1,0:T(8,128)(2,1)} %collective-permute-done.3), channel_id=1, source_target_pairs={{0,4},{4,0},{8,12},{12,8},{16,20},{20,16},{24,28},{28,24},{1,5},{5... | collective-permute-start | bytes 1572872 | tf_op jit(solution)/shard_map/ppermute | solution.py:34
  32.9 41.3 %collective-permute-start.10 = (bf16[320,512]{1,0:T(8,128)(2,1)}, bf16[320,512]{1,0:T(8,128)(2,1)}, u32[]{:S(2)}, u32[]{:S(2)}) collective-permute-start(bf16[320,512]{1,0:T(8,128)(2,1)} %get-tuple-element.6), channel_id=1, source_target_pairs={{0,2},{1,3},{2,0},{3,1},{4,6},{5,7},{6,4},{7,5},{8,10},{9,11},{10,... | collective-permute-start | bytes 983048 | tf_op jit(solution)/shard_map/ppermute | solution.py:122
  35.5 10.7 %collective-permute-start.6 = (bf16[1024,256]{1,0:T(8,128)(2,1)}, bf16[1024,256]{1,0:T(8,128)(2,1)S(1)}, u32[]{:S(2)}, u32[]{:S(2)}) collective-permute-start(bf16[1024,256]{1,0:T(8,128)(2,1)} %collective-permute-done.5), channel_id=1, source_target_pairs={{0,4},{4,0},{8,12},{12,8},{16,20},{20,16},{24,28},{28,24},{1,5},{5... | collective-permute-start | bytes 1572872 | tf_op jit(solution)/shard_map/ppermute | solution.py:34
  39.5 36.1 %collective-permute-start.12 = (bf16[320,512]{1,0:T(8,128)(2,1)S(1)}, bf16[320,512]{1,0:T(8,128)(2,1)}, u32[]{:S(2)}, u32[]{:S(2)}) collective-permute-start(bf16[320,512]{1,0:T(8,128)(2,1)S(1)} %copy-done.3), channel_id=1, source_target_pairs={{0,3},{1,2},{2,1},{3,0},{4,7},{5,6},{6,5},{7,4},{8,11},{9,10},{10,... | collective-permute-start | bytes 983048 | tf_op jit(solution)/shard_map/ppermute | solution.py:122
  57.1 20.4 %copy-start.4 = (bf16[256,512]{1,0:T(8,128)(2,1)S(1)}, bf16[256,512]{1,0:T(8,128)(2,1)}, u32[]{:S(2)}) copy-start(bf16[256,512]{1,0:T(8,128)(2,1)} %param.10) | copy-start | bytes 786436
  58.7 35.8 %copy-start.6 = (bf16[2048]{0:T(1024)(128)(2,1)S(1)}, bf16[2048]{0:T(1024)(128)(2,1)}, u32[]{:S(2)}) copy-start(bf16[2048]{0:T(1024)(128)(2,1)} %param.15) | copy-start | bytes 12292
  61.2 11.7 %collective-permute-start.7 = (bf16[256,320]{0,1:T(8,128)(2,1)S(1)}, bf16[256,320]{0,1:T(8,128)(2,1)S(1)}, u32[]{:S(2)}, u32[]{:S(2)}) collective-permute-start(bf16[256,320]{0,1:T(8,128)(2,1)S(1)} %select_select_fusion), channel_id=1, source_target_pairs={{0,1},{1,0},{2,3},{3,2},{4,5},{5,4},{6,7},{7,6},{8,9},{9,8},{10,11... | collective-permute-start | bytes 491528 | tf_op jit(solution)/shard_map/ppermute | solution.py:122
  61.5 10.8 %collective-permute-start.9 = (bf16[256,320]{0,1:T(8,128)(2,1)S(1)}, bf16[256,320]{0,1:T(8,128)(2,1)S(1)}, u32[]{:S(2)}, u32[]{:S(2)}) collective-permute-start(bf16[256,320]{0,1:T(8,128)(2,1)S(1)} %select_select_fusion), channel_id=1, source_target_pairs={{0,2},{1,3},{2,0},{3,1},{4,6},{5,7},{6,4},{7,5},{8,10},{9,11},{10,... | collective-permute-start | bytes 491528 | tf_op jit(solution)/shard_map/ppermute | solution.py:122
  72.3 5.3 %collective-permute-start.11 = (bf16[256,320]{0,1:T(8,128)(2,1)S(1)}, bf16[256,320]{0,1:T(8,128)(2,1)S(1)}, u32[]{:S(2)}, u32[]{:S(2)}) collective-permute-start(bf16[256,320]{0,1:T(8,128)(2,1)S(1)} %collective-permute-done.9), channel_id=1, source_target_pairs={{0,1},{1,0},{2,3},{3,2},{4,5},{5,4},{6,7},{7,6},{8,9},{9,8},{10,11... | collective-permute-start | bytes 491528 | tf_op jit(solution)/shard_map/ppermute | solution.py:122
  79.0 24.5 %copy-start.1 = (bf16[256,512]{1,0:T(8,128)(2,1)}, bf16[256,512]{1,0:T(8,128)(2,1)S(1)}, u32[]{:S(2)}) copy-start(bf16[256,512]{1,0:T(8,128)(2,1)S(1)} %get-tuple-element.48) | copy-start | bytes 786436
  79.0 14.9 %collective-permute-start.14 = (bf16[256,512]{1,0:T(8,128)(2,1)S(1)}, bf16[256,512]{1,0:T(8,128)(2,1)S(1)}, u32[]{:S(2)}, u32[]{:S(2)}) collective-permute-start(bf16[256,512]{1,0:T(8,128)(2,1)S(1)} %get-tuple-element.48), channel_id=1, source_target_pairs={{0,2},{1,3},{2,0},{3,1},{4,6},{5,7},{6,4},{7,5},{8,10},{9,11},{10,... | collective-permute-start | bytes 786440 | tf_op jit(solution)/shard_map/ppermute | solution.py:122
  82.2 12.5 %collective-permute-start.13 = (bf16[256,512]{1,0:T(8,128)(2,1)S(1)}, bf16[256,512]{1,0:T(8,128)(2,1)S(1)}, u32[]{:S(2)}, u32[]{:S(2)}) collective-permute-start(bf16[256,512]{1,0:T(8,128)(2,1)S(1)} %get-tuple-element.48), channel_id=1, source_target_pairs={{0,1},{1,0},{2,3},{3,2},{4,5},{5,4},{6,7},{7,6},{8,9},{9,8},{10,11... | collective-permute-start | bytes 786440 | tf_op jit(solution)/shard_map/ppermute | solution.py:122
  93.9 7.3 %collective-permute-start.15 = (bf16[256,512]{1,0:T(8,128)(2,1)S(1)}, bf16[256,512]{1,0:T(8,128)(2,1)S(1)}, u32[]{:S(2)}, u32[]{:S(2)}) collective-permute-start(bf16[256,512]{1,0:T(8,128)(2,1)S(1)} %collective-permute-done.14), channel_id=1, source_target_pairs={{0,1},{1,0},{2,3},{3,2},{4,5},{5,4},{6,7},{7,6},{8,9},{9,8},{10,11... | collective-permute-start | bytes 786440 | tf_op jit(solution)/shard_map/ppermute | solution.py:122
